TPU v7x, 512 devices: a whole 4x8x8 slice. The times are simulated.
512 devices in a mesh: ctx: 128 (over y, z, core), tp: 4 (over x).
Axes of the slice: x: 4, y: 8, z: 8, core: 2. Of those that a mesh axis runs over, the one named last changes fastest.
Arguments:
- outer_gate: bfloat16 [32768, 2048], P('ctx', 'tp'), may hold values from -6 to 6
- inner_gate: bfloat16 [32768, 2048], P('ctx', 'tp'), may hold values from -6 to 6
- stream: bfloat16 [32768, 2048], P('ctx', 'tp'), may hold values from -6 to 6
- filters: bfloat16 [128, 128], P('tp'), may hold values from -1 to 1
- query_rows: bfloat16 [32768, 2048], P('ctx', 'tp'), may hold values from -49 to 49
- key_rows: bfloat16 [32768, 2048], P('ctx', 'tp'), may hold values from -4 to 4
Outputs:
- mixed: bfloat16 [32768, 2048], P('ctx', 'tp')
- attended: bfloat16 [32768, 2048], P('ctx', 'tp')
All inputs are finite; a program needn't handle non-finite values.
Results may differ from a plain program's by a relative error of at most 0.007.
Values may be sent and summed in bfloat16 or wider, within the bound.
No kernel may reach another device: no remote copies, remote signals or barrier semaphores. Data moves between devices by JAX's collectives and lax.ppermute only.
A program may use at most 64 MiB of HBM per device.

v0:
```python
import math

import jax
import jax.numpy as jnp
from jax import lax
from jax.sharding import PartitionSpec as P

HEAD_DIM = 128


NEGATIVE = -1e30


def passed_along(block, axis, distance):
    devices = range(lax.axis_size(axis))
    route = [(i - distance, i) for i in devices if i - distance in devices]
    return lax.ppermute(block, axis, route)


def toeplitz_taps(filters, offset):
    kernel = filters.shape[1]
    tap_lags = (
        jnp.arange(kernel, dtype=jnp.int32)[:, None]
        - jnp.arange(kernel, dtype=jnp.int32)[None, :]
        + offset
    )
    in_range = (tap_lags >= 0) & (tap_lags < kernel)
    picked = jnp.take(filters, jnp.clip(tap_lags, 0, kernel - 1), axis=1)
    return jnp.where(in_range[None], picked, jnp.zeros_like(picked))


def apply_blocks(matrix, blocks):
    return jnp.einsum("gts,bsgc->btgc", matrix, blocks, preferred_element_type=jnp.float32)


def body(outer_gate, inner_gate, stream, filters, query_rows, key_rows):
    row_count, channels = outer_gate.shape
    groups, kernel = filters.shape
    group_size = channels // groups
    seq_span = min(8192 // row_count, lax.axis_size("ctx") // 2)
    half_span = seq_span // 2
    shard_index = lax.axis_index("ctx")
    seq_place = (shard_index + half_span) % seq_span
    product = (inner_gate.astype(jnp.float32) * stream.astype(jnp.float32)).astype(jnp.bfloat16)
    blocks = product.reshape(row_count // kernel, kernel, groups, group_size)
    near_taps = toeplitz_taps(filters, 0)
    far_taps = toeplitz_taps(filters, kernel)
    tail_rows = product[row_count - kernel + 1 :]
    earlier = passed_along(tail_rows, "ctx", 1)
    earlier = jnp.where(seq_place == 0, jnp.zeros_like(earlier), earlier)
    first_block = jnp.concatenate([jnp.zeros((1, channels), jnp.bfloat16), earlier], 0)
    first_block = first_block.reshape(1, kernel, groups, group_size)
    before = jnp.concatenate([first_block, blocks[:-1]], 0)
    filtered = (apply_blocks(near_taps, blocks) + apply_blocks(far_taps, before)).reshape(
        row_count, channels
    )
    mixed = (outer_gate.astype(jnp.float32) * filtered).astype(jnp.bfloat16)
    local_heads = channels // HEAD_DIM
    queries = query_rows.reshape(row_count, local_heads, HEAD_DIM)
    score_scale = 1.0 / math.sqrt(HEAD_DIM)
    query_pos = shard_index * row_count + jnp.arange(row_count, dtype=jnp.int32)
    seq_start = jnp.maximum(shard_index - seq_place, 0) * row_count
    win_shards = 2
    win_shards = min(win_shards, seq_span)
    kv_rows = jnp.stack([key_rows, mixed])
    reached = 1
    while reached < win_shards:
        arrived = passed_along(kv_rows, "ctx", reached)
        kv_rows = jnp.concatenate([arrived, kv_rows], 1)
        reached = reached * 2

    def attend(attn_state, window, first_shard):
        window_rows = window.shape[1]
        step_rows = min(512, window_rows)
        block_count = window_rows // step_rows
        split_window = window.reshape(2, block_count, step_rows, local_heads, HEAD_DIM)
        starts = first_shard * row_count + jnp.arange(block_count, dtype=jnp.int32) * step_rows

        def one_block(carried, block_item):
            key_block, value_block, key_start = block_item
            weighted, row_peak, row_total = carried
            scores = (
                jnp.einsum("qhd,khd->hqk", queries, key_block, preferred_element_type=jnp.float32)
                * score_scale
            )
            key_pos = key_start + jnp.arange(step_rows, dtype=jnp.int32)
            visible_keys = (key_pos[None, :] >= seq_start) & (
                key_pos[None, :] <= query_pos[:, None]
            )
            scores = jnp.where(visible_keys[None], scores, NEGATIVE)
            new_peak = jnp.maximum(row_peak, jnp.max(scores, axis=2))
            exp_terms = jnp.where(visible_keys[None], jnp.exp(scores - new_peak[..., None]), 0.0)
            rescale = jnp.exp(row_peak - new_peak)
            row_total = row_total * rescale + jnp.sum(exp_terms, axis=2)
            weights = exp_terms.astype(jnp.bfloat16)
            weighted = weighted * rescale[..., None] + jnp.einsum(
                "hqk,khd->hqd", weights, value_block, preferred_element_type=jnp.float32
            )
            return ((weighted, new_peak, row_total), None)

        attn_state, unused = lax.scan(
            one_block, attn_state, (split_window[0], split_window[1], starts)
        )
        return attn_state

    def visit(attn_state, window, first_shard):
        return attend(attn_state, window, first_shard)

    attn_state = (
        jnp.zeros((local_heads, row_count, HEAD_DIM), jnp.float32),
        jnp.full((local_heads, row_count), NEGATIVE, jnp.float32),
        jnp.zeros((local_heads, row_count), jnp.float32),
    )
    attn_state = visit(attn_state, kv_rows, shard_index - (win_shards - 1))

    def relay(turn_index, carried):
        window, held_state = carried
        window = passed_along(window, "ctx", win_shards)
        first_shard = shard_index - win_shards * (turn_index + 1) - (win_shards - 1)
        return (window, visit(held_state, window, first_shard))

    kv_rows, attn_state = lax.fori_loop(0, seq_span // win_shards - 1, relay, (kv_rows, attn_state))
    weighted, row_peak, row_total = attn_state
    attended = (
        (weighted / row_total[..., None])
        .transpose(1, 0, 2)
        .reshape(row_count, channels)
        .astype(jnp.bfloat16)
    )
    return (mixed, attended)


def solution(mesh):
    in_specs = (
        P("ctx", "tp"),
        P("ctx", "tp"),
        P("ctx", "tp"),
        P("tp", None),
        P("ctx", "tp"),
        P("ctx", "tp"),
    )
    out_specs = (P("ctx", "tp"), P("ctx", "tp"))
    return jax.shard_map(body, mesh=mesh, in_specs=in_specs, out_specs=out_specs, check_vma=False)
```

profile of v0, /device:TPU:32, one launch (start us, length us, event | category | flops | bytes accessed | tf_op | source)
XLA Modules:
  0.0 551.4 jit_solution(2223206030382744868)
XLA Ops:
  1.8 1.9 collective-permute-start.1
  4.8 57.8 %gather_fusion = bf16[16384,32]{1,0:T(8,128)(2,1)} fusion(bf16[32,128]{0,1:T(8,128)(2,1)S(1)} %copy.21, s32[16384]{0:T(1024)S(1)} %bitcast_clamp_fusion.1), kind=kCustom, calls=%fused_computation.clone | custom fusion | bytes 2162688 | tf_op jit(solution)/shard_map/jit(_take)/gather | solution.py:28
  62.6 4.0 copy.22
  67.4 57.8 %gather_fusion.1 = bf16[16384,32]{1,0:T(8,128)(2,1)} fusion(bf16[32,128]{0,1:T(8,128)(2,1)S(1)} %copy.21, s32[16384]{0:T(1024)S(1)} %bitcast_clamp_fusion), kind=kCustom, calls=%fused_computation.1.clone | custom fusion | bytes 2162688 | tf_op jit(solution)/shard_map/jit(_take)/gather | solution.py:28
  125.2 4.1 copy.27
  131.5 4.4 collective-permute-start.2
  136.9 11.6 %collective-permute-done.2 = bf16[2,256,512]{1,2,0:T(8,128)(2,1)S(1)} collective-permute-done((bf16[2,256,512]{1,2,0:T(8,128)(2,1)S(1)}, bf16[2,256,512]{1,2,0:T(8,128)(2,1)S(1)}, u32[]{:S(2)}, u32[]{:S(2)}) %collective-permute-start.2) | collective-permute-done | bytes 524320 | tf_op jit(solution)/shard_map/ppermute | solution.py:17
  150.8 399.7 %while.42 = (s32[]{:T(128)}, bf16[2,512,512]{1,2,0:T(8,128)(2,1)S(1)}, f32[4,256,128]{2,1,0:T(8,128)S(1)}, f32[4,256]{1,0:T(4,128)S(1)}, f32[4,256]{1,0:T(4,128)...) while((s32[]{:T(128)}, ...), condition=%wide.region_5.7_spmd.clone, body=%wide.region_2.6_spmd.clone.sunk | while | flops 275779328 | bytes 17636580 | solution.py:122
  150.8 1.9 collective-permute-start
  152.9 22.7 %collective-permute-done = bf16[2,512,512]{1,2,0:T(8,128)(2,1)S(1)} collective-permute-done((bf16[2,512,512]{1,2,0:T(8,128)(2,1)S(1)}, bf16[2,512,512]{1,2,0:T(8,128)(2,1)S(1)}, u32[]{:S(2)}, u32[]{:S(2)}) %collective-permute-start) | collective-permute-done | bytes 1048608 | tf_op jit(solution)/shard_map/while/body/eval_jaxpr/ppermute | solution.py:17
  178.2 1.9 collective-permute-start
  180.3 22.4 %collective-permute-done = bf16[2,512,512]{1,2,0:T(8,128)(2,1)S(1)} collective-permute-done((bf16[2,512,512]{1,2,0:T(8,128)(2,1)S(1)}, bf16[2,512,512]{1,2,0:T(8,128)(2,1)S(1)}, u32[]{:S(2)}, u32[]{:S(2)}) %collective-permute-start) | collective-permute-done | bytes 1048608 | tf_op jit(solution)/shard_map/while/body/eval_jaxpr/ppermute | solution.py:17
  205.2 3.0 collective-permute-start
  208.5 22.2 %collective-permute-done = bf16[2,512,512]{1,2,0:T(8,128)(2,1)S(1)} collective-permute-done((bf16[2,512,512]{1,2,0:T(8,128)(2,1)S(1)}, bf16[2,512,512]{1,2,0:T(8,128)(2,1)S(1)}, u32[]{:S(2)}, u32[]{:S(2)}) %collective-permute-start) | collective-permute-done | bytes 1048608 | tf_op jit(solution)/shard_map/while/body/eval_jaxpr/ppermute | solution.py:17
  233.2 4.1 collective-permute-start
  237.5 24.3 %collective-permute-done = bf16[2,512,512]{1,2,0:T(8,128)(2,1)S(1)} collective-permute-done((bf16[2,512,512]{1,2,0:T(8,128)(2,1)S(1)}, bf16[2,512,512]{1,2,0:T(8,128)(2,1)S(1)}, u32[]{:S(2)}, u32[]{:S(2)}) %collective-permute-start) | collective-permute-done | bytes 1048608 | tf_op jit(solution)/shard_map/while/body/eval_jaxpr/ppermute | solution.py:17
  264.4 1.9 collective-permute-start
  266.5 25.6 %collective-permute-done = bf16[2,512,512]{1,2,0:T(8,128)(2,1)S(1)} collective-permute-done((bf16[2,512,512]{1,2,0:T(8,128)(2,1)S(1)}, bf16[2,512,512]{1,2,0:T(8,128)(2,1)S(1)}, u32[]{:S(2)}, u32[]{:S(2)}) %collective-permute-start) | collective-permute-done | bytes 1048608 | tf_op jit(solution)/shard_map/while/body/eval_jaxpr/ppermute | solution.py:17
  294.6 1.9 collective-permute-start
  296.8 24.7 %collective-permute-done = bf16[2,512,512]{1,2,0:T(8,128)(2,1)S(1)} collective-permute-done((bf16[2,512,512]{1,2,0:T(8,128)(2,1)S(1)}, bf16[2,512,512]{1,2,0:T(8,128)(2,1)S(1)}, u32[]{:S(2)}, u32[]{:S(2)}) %collective-permute-start) | collective-permute-done | bytes 1048608 | tf_op jit(solution)/shard_map/while/body/eval_jaxpr/ppermute | solution.py:17
  324.0 1.9 collective-permute-start
  326.1 23.7 %collective-permute-done = bf16[2,512,512]{1,2,0:T(8,128)(2,1)S(1)} collective-permute-done((bf16[2,512,512]{1,2,0:T(8,128)(2,1)S(1)}, bf16[2,512,512]{1,2,0:T(8,128)(2,1)S(1)}, u32[]{:S(2)}, u32[]{:S(2)}) %collective-permute-start) | collective-permute-done | bytes 1048608 | tf_op jit(solution)/shard_map/while/body/eval_jaxpr/ppermute | solution.py:17
  354.5 22.8 %collective-permute-done = bf16[2,512,512]{1,2,0:T(8,128)(2,1)S(1)} collective-permute-done((bf16[2,512,512]{1,2,0:T(8,128)(2,1)S(1)}, bf16[2,512,512]{1,2,0:T(8,128)(2,1)S(1)}, u32[]{:S(2)}, u32[]{:S(2)}) %collective-permute-start) | collective-permute-done | bytes 1048608 | tf_op jit(solution)/shard_map/while/body/eval_jaxpr/ppermute | solution.py:17
  382.0 21.9 %collective-permute-done = bf16[2,512,512]{1,2,0:T(8,128)(2,1)S(1)} collective-permute-done((bf16[2,512,512]{1,2,0:T(8,128)(2,1)S(1)}, bf16[2,512,512]{1,2,0:T(8,128)(2,1)S(1)}, u32[]{:S(2)}, u32[]{:S(2)}) %collective-permute-start) | collective-permute-done | bytes 1048608 | tf_op jit(solution)/shard_map/while/body/eval_jaxpr/ppermute | solution.py:17
  408.6 21.0 %collective-permute-done = bf16[2,512,512]{1,2,0:T(8,128)(2,1)S(1)} collective-permute-done((bf16[2,512,512]{1,2,0:T(8,128)(2,1)S(1)}, bf16[2,512,512]{1,2,0:T(8,128)(2,1)S(1)}, u32[]{:S(2)}, u32[]{:S(2)}) %collective-permute-start) | collective-permute-done | bytes 1048608 | tf_op jit(solution)/shard_map/while/body/eval_jaxpr/ppermute | solution.py:17
  434.2 20.0 %collective-permute-done = bf16[2,512,512]{1,2,0:T(8,128)(2,1)S(1)} collective-permute-done((bf16[2,512,512]{1,2,0:T(8,128)(2,1)S(1)}, bf16[2,512,512]{1,2,0:T(8,128)(2,1)S(1)}, u32[]{:S(2)}, u32[]{:S(2)}) %collective-permute-start) | collective-permute-done | bytes 1048608 | tf_op jit(solution)/shard_map/while/body/eval_jaxpr/ppermute | solution.py:17
  458.9 19.1 %collective-permute-done = bf16[2,512,512]{1,2,0:T(8,128)(2,1)S(1)} collective-permute-done((bf16[2,512,512]{1,2,0:T(8,128)(2,1)S(1)}, bf16[2,512,512]{1,2,0:T(8,128)(2,1)S(1)}, u32[]{:S(2)}, u32[]{:S(2)}) %collective-permute-start) | collective-permute-done | bytes 1048608 | tf_op jit(solution)/shard_map/while/body/eval_jaxpr/ppermute | solution.py:17
  480.6 1.9 collective-permute-start
  482.7 18.6 %collective-permute-done = bf16[2,512,512]{1,2,0:T(8,128)(2,1)S(1)} collective-permute-done((bf16[2,512,512]{1,2,0:T(8,128)(2,1)S(1)}, bf16[2,512,512]{1,2,0:T(8,128)(2,1)S(1)}, u32[]{:S(2)}, u32[]{:S(2)}) %collective-permute-start) | collective-permute-done | bytes 1048608 | tf_op jit(solution)/shard_map/while/body/eval_jaxpr/ppermute | solution.py:17
  503.9 1.9 collective-permute-start
  506.1 19.4 %collective-permute-done = bf16[2,512,512]{1,2,0:T(8,128)(2,1)S(1)} collective-permute-done((bf16[2,512,512]{1,2,0:T(8,128)(2,1)S(1)}, bf16[2,512,512]{1,2,0:T(8,128)(2,1)S(1)}, u32[]{:S(2)}, u32[]{:S(2)}) %collective-permute-start) | collective-permute-done | bytes 1048608 | tf_op jit(solution)/shard_map/while/body/eval_jaxpr/ppermute | solution.py:17
  530.1 17.9 %collective-permute-done = bf16[2,512,512]{1,2,0:T(8,128)(2,1)S(1)} collective-permute-done((bf16[2,512,512]{1,2,0:T(8,128)(2,1)S(1)}, bf16[2,512,512]{1,2,0:T(8,128)(2,1)S(1)}, u32[]{:S(2)}, u32[]{:S(2)}) %collective-permute-start) | collective-permute-done | bytes 1048608 | tf_op jit(solution)/shard_map/while/body/eval_jaxpr/ppermute | solution.py:17
  (232 shorter events, 60.6 us)
Async XLA Ops:
  1.7 65.6 %copy-start = (bf16[256,512]{1,0:T(8,128)(2,1)}, bf16[256,512]{1,0:T(8,128)(2,1)S(1)}, u32[]{:S(2)}) copy-start(bf16[256,512]{1,0:T(8,128)(2,1)S(1)} %multiply_convert_fusion) | copy-start | bytes 786436
  1.8 128.3 %collective-permute-start.1 = (bf16[127,512]{1,0:T(8,128)(2,1)S(1)}, bf16[127,512]{1,0:T(8,128)(2,1)S(1)}, u32[]{:S(2)}, u32[]{:S(2)}) collective-permute-start(bf16[127,512]{1,0:T(8,128)(2,1)S(1)} %slice.52), channel_id=1, source_target_pairs={{0,4},{4,8},{8,12},{12,16},{16,20},{20,24},{24,28},{28,32},{32,36}... | collective-permute-start | bytes 390152 | tf_op jit(solution)/shard_map/ppermute | solution.py:17
  125.2 4.1 slice-start
  125.2 4.2 copy-start.1
  125.2 4.4 copy-start.2
  125.2 4.5 copy-start.3
  131.5 17.1 %collective-permute-start.2 = (bf16[2,256,512]{1,2,0:T(8,128)(2,1)S(1)}, bf16[2,256,512]{1,2,0:T(8,128)(2,1)S(1)}, u32[]{:S(2)}, u32[]{:S(2)}) collective-permute-start(bf16[2,256,512]{1,2,0:T(8,128)(2,1)S(1)} %pad_maximum_fusion), channel_id=1, source_target_pairs={{0,4},{4,8},{8,12},{12,16},{16,20},{20,24},{24,28},{28,32},{32,36}... | collective-permute-start | bytes 1572872 | tf_op jit(solution)/shard_map/ppermute | solution.py:17
  150.8 24.9 %collective-permute-start = (bf16[2,512,512]{1,2,0:T(8,128)(2,1)S(1)}, bf16[2,512,512]{1,2,0:T(8,128)(2,1)S(1)}, u32[]{:S(2)}, u32[]{:S(2)}) collective-permute-start(bf16[2,512,512]{1,2,0:T(8,128)(2,1)S(1)} %get-tuple-element.453), channel_id=1, source_target_pairs={{0,8},{4,12},{8,16},{12,20},{16,24},{20,28},{24,32},{28,36},{32,40... | collective-permute-start | bytes 3145736 | tf_op jit(solution)/shard_map/while/body/eval_jaxpr/ppermute | solution.py:17
  178.2 24.5 %collective-permute-start = (bf16[2,512,512]{1,2,0:T(8,128)(2,1)S(1)}, bf16[2,512,512]{1,2,0:T(8,128)(2,1)S(1)}, u32[]{:S(2)}, u32[]{:S(2)}) collective-permute-start(bf16[2,512,512]{1,2,0:T(8,128)(2,1)S(1)} %get-tuple-element.453), channel_id=1, source_target_pairs={{0,8},{4,12},{8,16},{12,20},{16,24},{20,28},{24,32},{28,36},{32,40... | collective-permute-start | bytes 3145736 | tf_op jit(solution)/shard_map/while/body/eval_jaxpr/ppermute | solution.py:17
  205.2 25.4 %collective-permute-start = (bf16[2,512,512]{1,2,0:T(8,128)(2,1)S(1)}, bf16[2,512,512]{1,2,0:T(8,128)(2,1)S(1)}, u32[]{:S(2)}, u32[]{:S(2)}) collective-permute-start(bf16[2,512,512]{1,2,0:T(8,128)(2,1)S(1)} %get-tuple-element.453), channel_id=1, source_target_pairs={{0,8},{4,12},{8,16},{12,20},{16,24},{20,28},{24,32},{28,36},{32,40... | collective-permute-start | bytes 3145736 | tf_op jit(solution)/shard_map/while/body/eval_jaxpr/ppermute | solution.py:17
  233.2 28.6 %collective-permute-start = (bf16[2,512,512]{1,2,0:T(8,128)(2,1)S(1)}, bf16[2,512,512]{1,2,0:T(8,128)(2,1)S(1)}, u32[]{:S(2)}, u32[]{:S(2)}) collective-permute-start(bf16[2,512,512]{1,2,0:T(8,128)(2,1)S(1)} %get-tuple-element.453), channel_id=1, source_target_pairs={{0,8},{4,12},{8,16},{12,20},{16,24},{20,28},{24,32},{28,36},{32,40... | collective-permute-start | bytes 3145736 | tf_op jit(solution)/shard_map/while/body/eval_jaxpr/ppermute | solution.py:17
  264.4 27.7 %collective-permute-start = (bf16[2,512,512]{1,2,0:T(8,128)(2,1)S(1)}, bf16[2,512,512]{1,2,0:T(8,128)(2,1)S(1)}, u32[]{:S(2)}, u32[]{:S(2)}) collective-permute-start(bf16[2,512,512]{1,2,0:T(8,128)(2,1)S(1)} %get-tuple-element.453), channel_id=1, source_target_pairs={{0,8},{4,12},{8,16},{12,20},{16,24},{20,28},{24,32},{28,36},{32,40... | collective-permute-start | bytes 3145736 | tf_op jit(solution)/shard_map/while/body/eval_jaxpr/ppermute | solution.py:17
  294.6 26.8 %collective-permute-start = (bf16[2,512,512]{1,2,0:T(8,128)(2,1)S(1)}, bf16[2,512,512]{1,2,0:T(8,128)(2,1)S(1)}, u32[]{:S(2)}, u32[]{:S(2)}) collective-permute-start(bf16[2,512,512]{1,2,0:T(8,128)(2,1)S(1)} %get-tuple-element.453), channel_id=1, source_target_pairs={{0,8},{4,12},{8,16},{12,20},{16,24},{20,28},{24,32},{28,36},{32,40... | collective-permute-start | bytes 3145736 | tf_op jit(solution)/shard_map/while/body/eval_jaxpr/ppermute | solution.py:17
  324.0 25.9 %collective-permute-start = (bf16[2,512,512]{1,2,0:T(8,128)(2,1)S(1)}, bf16[2,512,512]{1,2,0:T(8,128)(2,1)S(1)}, u32[]{:S(2)}, u32[]{:S(2)}) collective-permute-start(bf16[2,512,512]{1,2,0:T(8,128)(2,1)S(1)} %get-tuple-element.453), channel_id=1, source_target_pairs={{0,8},{4,12},{8,16},{12,20},{16,24},{20,28},{24,32},{28,36},{32,40... | collective-permute-start | bytes 3145736 | tf_op jit(solution)/shard_map/while/body/eval_jaxpr/ppermute | solution.py:17
  352.4 25.0 %collective-permute-start = (bf16[2,512,512]{1,2,0:T(8,128)(2,1)S(1)}, bf16[2,512,512]{1,2,0:T(8,128)(2,1)S(1)}, u32[]{:S(2)}, u32[]{:S(2)}) collective-permute-start(bf16[2,512,512]{1,2,0:T(8,128)(2,1)S(1)} %get-tuple-element.453), channel_id=1, source_target_pairs={{0,8},{4,12},{8,16},{12,20},{16,24},{20,28},{24,32},{28,36},{32,40... | collective-permute-start | bytes 3145736 | tf_op jit(solution)/shard_map/while/body/eval_jaxpr/ppermute | solution.py:17
  379.9 24.0 %collective-permute-start = (bf16[2,512,512]{1,2,0:T(8,128)(2,1)S(1)}, bf16[2,512,512]{1,2,0:T(8,128)(2,1)S(1)}, u32[]{:S(2)}, u32[]{:S(2)}) collective-permute-start(bf16[2,512,512]{1,2,0:T(8,128)(2,1)S(1)} %get-tuple-element.453), channel_id=1, source_target_pairs={{0,8},{4,12},{8,16},{12,20},{16,24},{20,28},{24,32},{28,36},{32,40... | collective-permute-start | bytes 3145736 | tf_op jit(solution)/shard_map/while/body/eval_jaxpr/ppermute | solution.py:17
  406.4 23.1 %collective-permute-start = (bf16[2,512,512]{1,2,0:T(8,128)(2,1)S(1)}, bf16[2,512,512]{1,2,0:T(8,128)(2,1)S(1)}, u32[]{:S(2)}, u32[]{:S(2)}) collective-permute-start(bf16[2,512,512]{1,2,0:T(8,128)(2,1)S(1)} %get-tuple-element.453), channel_id=1, source_target_pairs={{0,8},{4,12},{8,16},{12,20},{16,24},{20,28},{24,32},{28,36},{32,40... | collective-permute-start | bytes 3145736 | tf_op jit(solution)/shard_map/while/body/eval_jaxpr/ppermute | solution.py:17
  432.1 22.2 %collective-permute-start = (bf16[2,512,512]{1,2,0:T(8,128)(2,1)S(1)}, bf16[2,512,512]{1,2,0:T(8,128)(2,1)S(1)}, u32[]{:S(2)}, u32[]{:S(2)}) collective-permute-start(bf16[2,512,512]{1,2,0:T(8,128)(2,1)S(1)} %get-tuple-element.453), channel_id=1, source_target_pairs={{0,8},{4,12},{8,16},{12,20},{16,24},{20,28},{24,32},{28,36},{32,40... | collective-permute-start | bytes 3145736 | tf_op jit(solution)/shard_map/while/body/eval_jaxpr/ppermute | solution.py:17
  456.8 21.3 %collective-permute-start = (bf16[2,512,512]{1,2,0:T(8,128)(2,1)S(1)}, bf16[2,512,512]{1,2,0:T(8,128)(2,1)S(1)}, u32[]{:S(2)}, u32[]{:S(2)}) collective-permute-start(bf16[2,512,512]{1,2,0:T(8,128)(2,1)S(1)} %get-tuple-element.453), channel_id=1, source_target_pairs={{0,8},{4,12},{8,16},{12,20},{16,24},{20,28},{24,32},{28,36},{32,40... | collective-permute-start | bytes 3145736 | tf_op jit(solution)/shard_map/while/body/eval_jaxpr/ppermute | solution.py:17
  480.6 20.8 %collective-permute-start = (bf16[2,512,512]{1,2,0:T(8,128)(2,1)S(1)}, bf16[2,512,512]{1,2,0:T(8,128)(2,1)S(1)}, u32[]{:S(2)}, u32[]{:S(2)}) collective-permute-start(bf16[2,512,512]{1,2,0:T(8,128)(2,1)S(1)} %get-tuple-element.453), channel_id=1, source_target_pairs={{0,8},{4,12},{8,16},{12,20},{16,24},{20,28},{24,32},{28,36},{32,40... | collective-permute-start | bytes 3145736 | tf_op jit(solution)/shard_map/while/body/eval_jaxpr/ppermute | solution.py:17
  503.9 21.5 %collective-permute-start = (bf16[2,512,512]{1,2,0:T(8,128)(2,1)S(1)}, bf16[2,512,512]{1,2,0:T(8,128)(2,1)S(1)}, u32[]{:S(2)}, u32[]{:S(2)}) collective-permute-start(bf16[2,512,512]{1,2,0:T(8,128)(2,1)S(1)} %get-tuple-element.453), channel_id=1, source_target_pairs={{0,8},{4,12},{8,16},{12,20},{16,24},{20,28},{24,32},{28,36},{32,40... | collective-permute-start | bytes 3145736 | tf_op jit(solution)/shard_map/while/body/eval_jaxpr/ppermute | solution.py:17
  528.0 20.0 %collective-permute-start = (bf16[2,512,512]{1,2,0:T(8,128)(2,1)S(1)}, bf16[2,512,512]{1,2,0:T(8,128)(2,1)S(1)}, u32[]{:S(2)}, u32[]{:S(2)}) collective-permute-start(bf16[2,512,512]{1,2,0:T(8,128)(2,1)S(1)} %get-tuple-element.453), channel_id=1, source_target_pairs={{0,8},{4,12},{8,16},{12,20},{16,24},{20,28},{24,32},{28,36},{32,40... | collective-permute-start | bytes 3145736 | tf_op jit(solution)/shard_map/while/body/eval_jaxpr/ppermute | solution.py:17
where the time goes:
time: 552 us; the launch traced here: 551 us
  waiting for transfers between devices  338 us (61%)
  local copies, waits for them, and re-layouts  129 us (23%)
  starting transfers between devices  38.4 us (7%)
  matrix products  25.2 us (5%)
  other arithmetic  18.5 us (3%)
    ppermute x17, waiting for transfers between devices, passed_along(): return lax.ppermute(block, axis, route)  338 us
    gather x4, local copies, waits for them, and re-layouts, toeplitz_taps(): picked = jnp.take(filters, jnp.clip(tap_lags, 0, kernel - 1), axis=1)  124 us
    ppermute x17, starting transfers between devices, passed_along(): return lax.ppermute(block, axis, route)  38.4 us
    dot_general x16, matrix products, one_block(): jnp.einsum('hqk,khd->hqd', weights, value_block, preferred_element_type=j...  14.9 us
    reduce_sum x16, other arithmetic, one_block(): row_total = row_total * rescale + jnp.sum(exp_terms, axis=2)  12.9 us
  transfers between devices with their start and end apart: 17, of which 16 were waited for; matrix products, arithmetic and copies ran while one was open for 24% of the time, Pallas kernels for 0%

commit v1 on v0

--- a/solution.py
+++ b/solution.py
@@ -18,15 +18,13 @@
 
 
 def toeplitz_taps(filters, offset):
-    kernel = filters.shape[1]
-    tap_lags = (
-        jnp.arange(kernel, dtype=jnp.int32)[:, None]
-        - jnp.arange(kernel, dtype=jnp.int32)[None, :]
-        + offset
-    )
-    in_range = (tap_lags >= 0) & (tap_lags < kernel)
-    picked = jnp.take(filters, jnp.clip(tap_lags, 0, kernel - 1), axis=1)
-    return jnp.where(in_range[None], picked, jnp.zeros_like(picked))
+    groups, kernel = filters.shape
+    flipped = filters[:, ::-1]
+    zeros = jnp.zeros_like(flipped)
+    pieces = [flipped, zeros] if offset == 0 else [zeros, flipped]
+    lags = jnp.concatenate(pieces, axis=1)
+    flat = jnp.tile(lags, (1, kernel))[:, : kernel * (2 * kernel - 1)]
+    return flat.reshape(groups, kernel, 2 * kernel - 1)[:, :, kernel - 1 : 2 * kernel - 1]
 
 
 def apply_blocks(matrix, blocks):

time: 552 us -> 456 us (0.83)
  the two profiles are of different devices: /device:TPU:32 before, /device:TPU:38 now
where the time goes in v1:
time: 456 us; the launch traced here: 455 us
  waiting for transfers between devices  338 us (74%)
  starting transfers between devices  38.6 us (8%)
  local copies, waits for them, and re-layouts  29.6 us (6%)
  matrix products  27 us (6%)
  other arithmetic  19.9 us (4%)
    ppermute x17, waiting for transfers between devices, passed_along(): return lax.ppermute(block, axis, route)  338 us
    ppermute x17, starting transfers between devices, passed_along(): return lax.ppermute(block, axis, route)  38.6 us
    reshape x2, local copies, waits for them, and re-layouts, toeplitz_taps(): flat.reshape(groups, kernel, 2 * kernel - 1)  15.6 us
    dot_general x16, matrix products, one_block(): jnp.einsum('hqk,khd->hqd', weights, value_block, preferred_element_type=j...  14.9 us
    reduce_sum x16, other arithmetic, one_block(): row_total = row_total * rescale + jnp.sum(exp_terms, axis=2)  12.9 us
  transfers between devices with their start and end apart: 17, of which 16 were waited for; matrix products, arithmetic and copies ran while one was open for 6% of the time, Pallas kernels for 0%

profile of v1, /device:TPU:38, one launch (start us, length us, event | category | flops | bytes accessed | tf_op | source)
XLA Modules:
  0.0 455.4 jit_solution(6452019920765026704)
XLA Ops:
  6.8 7.8 %reshape.173 = bf16[32,128,255]{2,1,0:T(8,128)(2,1)} reshape(bf16[32,32640]{1,0:T(8,128)(2,1)S(1)} %slice.64) | data formatting | bytes 4177920 | tf_op jit(solution)/shard_map/reshape | solution.py:27
  14.7 2.3 fusion.17
  18.6 7.8 %reshape.175 = bf16[32,128,255]{2,1,0:T(8,128)(2,1)} reshape(bf16[32,32640]{1,0:T(8,128)(2,1)S(1)} %slice.68) | data formatting | bytes 4177920 | tf_op jit(solution)/shard_map/reshape | solution.py:27
  35.2 4.6 %collective-permute-start.2 = (bf16[2,256,512]{1,2,0:T(8,128)(2,1)S(1)}, bf16[2,256,512]{1,2,0:T(8,128)(2,1)S(1)}, u32[]{:S(2)}, u32[]{:S(2)}) collective-permute-start(bf16[2,256,512]{1,2,0:T(8,128)(2,1)S(1)} %pad_maximum_fusion), channel_id=1, source_target_pairs={{0,4},{4,8},{8,12},{12,16},{16,20},{20,24},{24,28},{28,32},{32,36}... | collective-permute-start | bytes 1572872 | tf_op jit(solution)/shard_map/ppermute | solution.py:17
  40.8 11.5 %collective-permute-done.2 = bf16[2,256,512]{1,2,0:T(8,128)(2,1)S(1)} collective-permute-done((bf16[2,256,512]{1,2,0:T(8,128)(2,1)S(1)}, bf16[2,256,512]{1,2,0:T(8,128)(2,1)S(1)}, u32[]{:S(2)}, u32[]{:S(2)}) %collective-permute-start.2) | collective-permute-done | bytes 524320 | tf_op jit(solution)/shard_map/ppermute | solution.py:17
  54.5 400.0 %while.42 = (s32[]{:T(128)}, bf16[2,512,512]{1,2,0:T(8,128)(2,1)S(1)}, f32[4,256,128]{2,1,0:T(8,128)S(1)}, f32[4,256]{1,0:T(4,128)S(1)}, f32[4,256]{1,0:T(4,128)...) while((s32[]{:T(128)}, ...), condition=%wide.region_5.6_spmd.clone, body=%wide.region_2.5_spmd.clone.sunk | while | flops 275779328 | bytes 17636580 | solution.py:120
  54.5 1.9 collective-permute-start
  56.6 22.7 %collective-permute-done = bf16[2,512,512]{1,2,0:T(8,128)(2,1)S(1)} collective-permute-done((bf16[2,512,512]{1,2,0:T(8,128)(2,1)S(1)}, bf16[2,512,512]{1,2,0:T(8,128)(2,1)S(1)}, u32[]{:S(2)}, u32[]{:S(2)}) %collective-permute-start) | collective-permute-done | bytes 1048608 | tf_op jit(solution)/shard_map/while/body/eval_jaxpr/ppermute | solution.py:17
  81.9 1.9 collective-permute-start
  84.1 22.4 %collective-permute-done = bf16[2,512,512]{1,2,0:T(8,128)(2,1)S(1)} collective-permute-done((bf16[2,512,512]{1,2,0:T(8,128)(2,1)S(1)}, bf16[2,512,512]{1,2,0:T(8,128)(2,1)S(1)}, u32[]{:S(2)}, u32[]{:S(2)}) %collective-permute-start) | collective-permute-done | bytes 1048608 | tf_op jit(solution)/shard_map/while/body/eval_jaxpr/ppermute | solution.py:17
  109.0 3.0 collective-permute-start
  112.2 22.1 %collective-permute-done = bf16[2,512,512]{1,2,0:T(8,128)(2,1)S(1)} collective-permute-done((bf16[2,512,512]{1,2,0:T(8,128)(2,1)S(1)}, bf16[2,512,512]{1,2,0:T(8,128)(2,1)S(1)}, u32[]{:S(2)}, u32[]{:S(2)}) %collective-permute-start) | collective-permute-done | bytes 1048608 | tf_op jit(solution)/shard_map/while/body/eval_jaxpr/ppermute | solution.py:17
  136.9 4.2 collective-permute-start
  141.3 24.3 %collective-permute-done = bf16[2,512,512]{1,2,0:T(8,128)(2,1)S(1)} collective-permute-done((bf16[2,512,512]{1,2,0:T(8,128)(2,1)S(1)}, bf16[2,512,512]{1,2,0:T(8,128)(2,1)S(1)}, u32[]{:S(2)}, u32[]{:S(2)}) %collective-permute-start) | collective-permute-done | bytes 1048608 | tf_op jit(solution)/shard_map/while/body/eval_jaxpr/ppermute | solution.py:17
  168.1 1.9 collective-permute-start
  170.2 25.6 %collective-permute-done = bf16[2,512,512]{1,2,0:T(8,128)(2,1)S(1)} collective-permute-done((bf16[2,512,512]{1,2,0:T(8,128)(2,1)S(1)}, bf16[2,512,512]{1,2,0:T(8,128)(2,1)S(1)}, u32[]{:S(2)}, u32[]{:S(2)}) %collective-permute-start) | collective-permute-done | bytes 1048608 | tf_op jit(solution)/shard_map/while/body/eval_jaxpr/ppermute | solution.py:17
  198.4 1.9 collective-permute-start
  200.5 24.7 %collective-permute-done = bf16[2,512,512]{1,2,0:T(8,128)(2,1)S(1)} collective-permute-done((bf16[2,512,512]{1,2,0:T(8,128)(2,1)S(1)}, bf16[2,512,512]{1,2,0:T(8,128)(2,1)S(1)}, u32[]{:S(2)}, u32[]{:S(2)}) %collective-permute-start) | collective-permute-done | bytes 1048608 | tf_op jit(solution)/shard_map/while/body/eval_jaxpr/ppermute | solution.py:17
  227.8 1.9 collective-permute-start
  229.9 23.8 %collective-permute-done = bf16[2,512,512]{1,2,0:T(8,128)(2,1)S(1)} collective-permute-done((bf16[2,512,512]{1,2,0:T(8,128)(2,1)S(1)}, bf16[2,512,512]{1,2,0:T(8,128)(2,1)S(1)}, u32[]{:S(2)}, u32[]{:S(2)}) %collective-permute-start) | collective-permute-done | bytes 1048608 | tf_op jit(solution)/shard_map/while/body/eval_jaxpr/ppermute | solution.py:17
  256.2 1.9 collective-permute-start
  258.4 22.9 %collective-permute-done = bf16[2,512,512]{1,2,0:T(8,128)(2,1)S(1)} collective-permute-done((bf16[2,512,512]{1,2,0:T(8,128)(2,1)S(1)}, bf16[2,512,512]{1,2,0:T(8,128)(2,1)S(1)}, u32[]{:S(2)}, u32[]{:S(2)}) %collective-permute-start) | collective-permute-done | bytes 1048608 | tf_op jit(solution)/shard_map/while/body/eval_jaxpr/ppermute | solution.py:17
  285.9 21.9 %collective-permute-done = bf16[2,512,512]{1,2,0:T(8,128)(2,1)S(1)} collective-permute-done((bf16[2,512,512]{1,2,0:T(8,128)(2,1)S(1)}, bf16[2,512,512]{1,2,0:T(8,128)(2,1)S(1)}, u32[]{:S(2)}, u32[]{:S(2)}) %collective-permute-start) | collective-permute-done | bytes 1048608 | tf_op jit(solution)/shard_map/while/body/eval_jaxpr/ppermute | solution.py:17
  312.5 21.0 %collective-permute-done = bf16[2,512,512]{1,2,0:T(8,128)(2,1)S(1)} collective-permute-done((bf16[2,512,512]{1,2,0:T(8,128)(2,1)S(1)}, bf16[2,512,512]{1,2,0:T(8,128)(2,1)S(1)}, u32[]{:S(2)}, u32[]{:S(2)}) %collective-permute-start) | collective-permute-done | bytes 1048608 | tf_op jit(solution)/shard_map/while/body/eval_jaxpr/ppermute | solution.py:17
  338.1 20.1 %collective-permute-done = bf16[2,512,512]{1,2,0:T(8,128)(2,1)S(1)} collective-permute-done((bf16[2,512,512]{1,2,0:T(8,128)(2,1)S(1)}, bf16[2,512,512]{1,2,0:T(8,128)(2,1)S(1)}, u32[]{:S(2)}, u32[]{:S(2)}) %collective-permute-start) | collective-permute-done | bytes 1048608 | tf_op jit(solution)/shard_map/while/body/eval_jaxpr/ppermute | solution.py:17
  360.8 1.9 collective-permute-start
  362.9 19.2 %collective-permute-done = bf16[2,512,512]{1,2,0:T(8,128)(2,1)S(1)} collective-permute-done((bf16[2,512,512]{1,2,0:T(8,128)(2,1)S(1)}, bf16[2,512,512]{1,2,0:T(8,128)(2,1)S(1)}, u32[]{:S(2)}, u32[]{:S(2)}) %collective-permute-start) | collective-permute-done | bytes 1048608 | tf_op jit(solution)/shard_map/while/body/eval_jaxpr/ppermute | solution.py:17
  384.6 1.9 collective-permute-start
  386.7 18.7 %collective-permute-done = bf16[2,512,512]{1,2,0:T(8,128)(2,1)S(1)} collective-permute-done((bf16[2,512,512]{1,2,0:T(8,128)(2,1)S(1)}, bf16[2,512,512]{1,2,0:T(8,128)(2,1)S(1)}, u32[]{:S(2)}, u32[]{:S(2)}) %collective-permute-start) | collective-permute-done | bytes 1048608 | tf_op jit(solution)/shard_map/while/body/eval_jaxpr/ppermute | solution.py:17
  407.9 1.9 collective-permute-start
  410.1 19.4 %collective-permute-done = bf16[2,512,512]{1,2,0:T(8,128)(2,1)S(1)} collective-permute-done((bf16[2,512,512]{1,2,0:T(8,128)(2,1)S(1)}, bf16[2,512,512]{1,2,0:T(8,128)(2,1)S(1)}, u32[]{:S(2)}, u32[]{:S(2)}) %collective-permute-start) | collective-permute-done | bytes 1048608 | tf_op jit(solution)/shard_map/while/body/eval_jaxpr/ppermute | solution.py:17
  434.1 17.9 %collective-permute-done = bf16[2,512,512]{1,2,0:T(8,128)(2,1)S(1)} collective-permute-done((bf16[2,512,512]{1,2,0:T(8,128)(2,1)S(1)}, bf16[2,512,512]{1,2,0:T(8,128)(2,1)S(1)}, u32[]{:S(2)}, u32[]{:S(2)}) %collective-permute-start) | collective-permute-done | bytes 1048608 | tf_op jit(solution)/shard_map/while/body/eval_jaxpr/ppermute | solution.py:17
  (233 shorter events, 68.2 us)
Async XLA Ops:
  1.7 15.3 %copy-start.1 = (bf16[256,512]{1,0:T(8,128)(2,1)}, bf16[256,512]{1,0:T(8,128)(2,1)S(1)}, u32[]{:S(2)}) copy-start(bf16[256,512]{1,0:T(8,128)(2,1)S(1)} %multiply_convert_fusion) | copy-start | bytes 786436
  2.5 27.2 %collective-permute-start.1 = (bf16[127,512]{1,0:T(8,128)(2,1)}, bf16[127,512]{1,0:T(8,128)(2,1)}, u32[]{:S(2)}, u32[]{:S(2)}) collective-permute-start(bf16[127,512]{1,0:T(8,128)(2,1)} %slice.66), channel_id=1, source_target_pairs={{0,4},{4,8},{8,12},{12,16},{16,20},{20,24},{24,28},{28,32},{32,36}... | collective-permute-start | bytes 390152 | tf_op jit(solution)/shard_map/ppermute | solution.py:17
  18.5 7.8 %slice-start = ((bf16[256,512]{1,0:T(8,128)(2,1)}), bf16[128,512]{1,0:T(8,128)(2,1)S(1)}, s32[]{:S(2)}) async-start(bf16[256,512]{1,0:T(8,128)(2,1)} %copy-done.1), calls=%async_computation | async-start | bytes 262144 | tf_op jit(solution)/shard_map/slice | solution.py:51
  18.5 7.9 %copy-start.3 = (bf16[256,512]{1,0:T(8,128)(2,1)S(1)}, bf16[256,512]{1,0:T(8,128)(2,1)}, u32[]{:S(2)}) copy-start(bf16[256,512]{1,0:T(8,128)(2,1)} %param.8) | copy-start | bytes 786436
  26.4 7.7 %copy-start = (bf16[32,128,255]{2,1,0:T(8,128)(2,1)S(1)}, bf16[32,128,255]{2,1,0:T(8,128)(2,1)}, u32[]{:S(2)}) copy-start(bf16[32,128,255]{2,1,0:T(8,128)(2,1)} %reshape.175) | copy-start | bytes 6266884
  33.0 2.1 copy-start.2
  35.2 17.1 %collective-permute-start.2 = (bf16[2,256,512]{1,2,0:T(8,128)(2,1)S(1)}, bf16[2,256,512]{1,2,0:T(8,128)(2,1)S(1)}, u32[]{:S(2)}, u32[]{:S(2)}) collective-permute-start(bf16[2,256,512]{1,2,0:T(8,128)(2,1)S(1)} %pad_maximum_fusion), channel_id=1, source_target_pairs={{0,4},{4,8},{8,12},{12,16},{16,20},{20,24},{24,28},{28,32},{32,36}... | collective-permute-start | bytes 1572872 | tf_op jit(solution)/shard_map/ppermute | solution.py:17
  54.5 24.9 %collective-permute-start = (bf16[2,512,512]{1,2,0:T(8,128)(2,1)S(1)}, bf16[2,512,512]{1,2,0:T(8,128)(2,1)S(1)}, u32[]{:S(2)}, u32[]{:S(2)}) collective-permute-start(bf16[2,512,512]{1,2,0:T(8,128)(2,1)S(1)} %get-tuple-element.450), channel_id=1, source_target_pairs={{0,8},{4,12},{8,16},{12,20},{16,24},{20,28},{24,32},{28,36},{32,40... | collective-permute-start | bytes 3145736 | tf_op jit(solution)/shard_map/while/body/eval_jaxpr/ppermute | solution.py:17
  81.9 24.5 %collective-permute-start = (bf16[2,512,512]{1,2,0:T(8,128)(2,1)S(1)}, bf16[2,512,512]{1,2,0:T(8,128)(2,1)S(1)}, u32[]{:S(2)}, u32[]{:S(2)}) collective-permute-start(bf16[2,512,512]{1,2,0:T(8,128)(2,1)S(1)} %get-tuple-element.450), channel_id=1, source_target_pairs={{0,8},{4,12},{8,16},{12,20},{16,24},{20,28},{24,32},{28,36},{32,40... | collective-permute-start | bytes 3145736 | tf_op jit(solution)/shard_map/while/body/eval_jaxpr/ppermute | solution.py:17
  109.0 25.4 %collective-permute-start = (bf16[2,512,512]{1,2,0:T(8,128)(2,1)S(1)}, bf16[2,512,512]{1,2,0:T(8,128)(2,1)S(1)}, u32[]{:S(2)}, u32[]{:S(2)}) collective-permute-start(bf16[2,512,512]{1,2,0:T(8,128)(2,1)S(1)} %get-tuple-element.450), channel_id=1, source_target_pairs={{0,8},{4,12},{8,16},{12,20},{16,24},{20,28},{24,32},{28,36},{32,40... | collective-permute-start | bytes 3145736 | tf_op jit(solution)/shard_map/while/body/eval_jaxpr/ppermute | solution.py:17
  136.9 28.7 %collective-permute-start = (bf16[2,512,512]{1,2,0:T(8,128)(2,1)S(1)}, bf16[2,512,512]{1,2,0:T(8,128)(2,1)S(1)}, u32[]{:S(2)}, u32[]{:S(2)}) collective-permute-start(bf16[2,512,512]{1,2,0:T(8,128)(2,1)S(1)} %get-tuple-element.450), channel_id=1, source_target_pairs={{0,8},{4,12},{8,16},{12,20},{16,24},{20,28},{24,32},{28,36},{32,40... | collective-permute-start | bytes 3145736 | tf_op jit(solution)/shard_map/while/body/eval_jaxpr/ppermute | solution.py:17
  168.1 27.8 %collective-permute-start = (bf16[2,512,512]{1,2,0:T(8,128)(2,1)S(1)}, bf16[2,512,512]{1,2,0:T(8,128)(2,1)S(1)}, u32[]{:S(2)}, u32[]{:S(2)}) collective-permute-start(bf16[2,512,512]{1,2,0:T(8,128)(2,1)S(1)} %get-tuple-element.450), channel_id=1, source_target_pairs={{0,8},{4,12},{8,16},{12,20},{16,24},{20,28},{24,32},{28,36},{32,40... | collective-permute-start | bytes 3145736 | tf_op jit(solution)/shard_map/while/body/eval_jaxpr/ppermute | solution.py:17
  198.4 26.8 %collective-permute-start = (bf16[2,512,512]{1,2,0:T(8,128)(2,1)S(1)}, bf16[2,512,512]{1,2,0:T(8,128)(2,1)S(1)}, u32[]{:S(2)}, u32[]{:S(2)}) collective-permute-start(bf16[2,512,512]{1,2,0:T(8,128)(2,1)S(1)} %get-tuple-element.450), channel_id=1, source_target_pairs={{0,8},{4,12},{8,16},{12,20},{16,24},{20,28},{24,32},{28,36},{32,40... | collective-permute-start | bytes 3145736 | tf_op jit(solution)/shard_map/while/body/eval_jaxpr/ppermute | solution.py:17
  227.8 25.9 %collective-permute-start = (bf16[2,512,512]{1,2,0:T(8,128)(2,1)S(1)}, bf16[2,512,512]{1,2,0:T(8,128)(2,1)S(1)}, u32[]{:S(2)}, u32[]{:S(2)}) collective-permute-start(bf16[2,512,512]{1,2,0:T(8,128)(2,1)S(1)} %get-tuple-element.450), channel_id=1, source_target_pairs={{0,8},{4,12},{8,16},{12,20},{16,24},{20,28},{24,32},{28,36},{32,40... | collective-permute-start | bytes 3145736 | tf_op jit(solution)/shard_map/while/body/eval_jaxpr/ppermute | solution.py:17
  256.2 25.0 %collective-permute-start = (bf16[2,512,512]{1,2,0:T(8,128)(2,1)S(1)}, bf16[2,512,512]{1,2,0:T(8,128)(2,1)S(1)}, u32[]{:S(2)}, u32[]{:S(2)}) collective-permute-start(bf16[2,512,512]{1,2,0:T(8,128)(2,1)S(1)} %get-tuple-element.450), channel_id=1, source_target_pairs={{0,8},{4,12},{8,16},{12,20},{16,24},{20,28},{24,32},{28,36},{32,40... | collective-permute-start | bytes 3145736 | tf_op jit(solution)/shard_map/while/body/eval_jaxpr/ppermute | solution.py:17
  283.7 24.1 %collective-permute-start = (bf16[2,512,512]{1,2,0:T(8,128)(2,1)S(1)}, bf16[2,512,512]{1,2,0:T(8,128)(2,1)S(1)}, u32[]{:S(2)}, u32[]{:S(2)}) collective-permute-start(bf16[2,512,512]{1,2,0:T(8,128)(2,1)S(1)} %get-tuple-element.450), channel_id=1, source_target_pairs={{0,8},{4,12},{8,16},{12,20},{16,24},{20,28},{24,32},{28,36},{32,40... | collective-permute-start | bytes 3145736 | tf_op jit(solution)/shard_map/while/body/eval_jaxpr/ppermute | solution.py:17
  310.3 23.1 %collective-permute-start = (bf16[2,512,512]{1,2,0:T(8,128)(2,1)S(1)}, bf16[2,512,512]{1,2,0:T(8,128)(2,1)S(1)}, u32[]{:S(2)}, u32[]{:S(2)}) collective-permute-start(bf16[2,512,512]{1,2,0:T(8,128)(2,1)S(1)} %get-tuple-element.450), channel_id=1, source_target_pairs={{0,8},{4,12},{8,16},{12,20},{16,24},{20,28},{24,32},{28,36},{32,40... | collective-permute-start | bytes 3145736 | tf_op jit(solution)/shard_map/while/body/eval_jaxpr/ppermute | solution.py:17
  336.0 22.2 %collective-permute-start = (bf16[2,512,512]{1,2,0:T(8,128)(2,1)S(1)}, bf16[2,512,512]{1,2,0:T(8,128)(2,1)S(1)}, u32[]{:S(2)}, u32[]{:S(2)}) collective-permute-start(bf16[2,512,512]{1,2,0:T(8,128)(2,1)S(1)} %get-tuple-element.450), channel_id=1, source_target_pairs={{0,8},{4,12},{8,16},{12,20},{16,24},{20,28},{24,32},{28,36},{32,40... | collective-permute-start | bytes 3145736 | tf_op jit(solution)/shard_map/while/body/eval_jaxpr/ppermute | solution.py:17
  360.8 21.3 %collective-permute-start = (bf16[2,512,512]{1,2,0:T(8,128)(2,1)S(1)}, bf16[2,512,512]{1,2,0:T(8,128)(2,1)S(1)}, u32[]{:S(2)}, u32[]{:S(2)}) collective-permute-start(bf16[2,512,512]{1,2,0:T(8,128)(2,1)S(1)} %get-tuple-element.450), channel_id=1, source_target_pairs={{0,8},{4,12},{8,16},{12,20},{16,24},{20,28},{24,32},{28,36},{32,40... | collective-permute-start | bytes 3145736 | tf_op jit(solution)/shard_map/while/body/eval_jaxpr/ppermute | solution.py:17
  384.6 20.8 %collective-permute-start = (bf16[2,512,512]{1,2,0:T(8,128)(2,1)S(1)}, bf16[2,512,512]{1,2,0:T(8,128)(2,1)S(1)}, u32[]{:S(2)}, u32[]{:S(2)}) collective-permute-start(bf16[2,512,512]{1,2,0:T(8,128)(2,1)S(1)} %get-tuple-element.450), channel_id=1, source_target_pairs={{0,8},{4,12},{8,16},{12,20},{16,24},{20,28},{24,32},{28,36},{32,40... | collective-permute-start | bytes 3145736 | tf_op jit(solution)/shard_map/while/body/eval_jaxpr/ppermute | solution.py:17
  407.9 21.5 %collective-permute-start = (bf16[2,512,512]{1,2,0:T(8,128)(2,1)S(1)}, bf16[2,512,512]{1,2,0:T(8,128)(2,1)S(1)}, u32[]{:S(2)}, u32[]{:S(2)}) collective-permute-start(bf16[2,512,512]{1,2,0:T(8,128)(2,1)S(1)} %get-tuple-element.450), channel_id=1, source_target_pairs={{0,8},{4,12},{8,16},{12,20},{16,24},{20,28},{24,32},{28,36},{32,40... | collective-permute-start | bytes 3145736 | tf_op jit(solution)/shard_map/while/body/eval_jaxpr/ppermute | solution.py:17
  432.0 20.0 %collective-permute-start = (bf16[2,512,512]{1,2,0:T(8,128)(2,1)S(1)}, bf16[2,512,512]{1,2,0:T(8,128)(2,1)S(1)}, u32[]{:S(2)}, u32[]{:S(2)}) collective-permute-start(bf16[2,512,512]{1,2,0:T(8,128)(2,1)S(1)} %get-tuple-element.450), channel_id=1, source_target_pairs={{0,8},{4,12},{8,16},{12,20},{16,24},{20,28},{24,32},{28,36},{32,40... | collective-permute-start | bytes 3145736 | tf_op jit(solution)/shard_map/while/body/eval_jaxpr/ppermute | solution.py:17

commit v2 on v1

v2 whole, which is shorter than its diff:
```python
import functools
import math

import jax
import jax.numpy as jnp
from jax import lax
from jax.sharding import Mesh, NamedSharding
from jax.sharding import PartitionSpec as P

HEAD_DIM = 128
LENGTH = 8192
CORES = 2
WINDOW_SHARDS = 8

NEGATIVE = -1e30
CTX_AXES = ("row", "col", "core")


def passed_along(block, axis, size, distance):
    route = [(i - distance, i) for i in range(size) if i - distance >= 0]
    return lax.ppermute(block, axis, route)


def toeplitz_taps(filters, offset):
    groups, kernel = filters.shape
    flipped = filters[:, ::-1]
    zeros = jnp.zeros_like(flipped)
    pieces = [flipped, zeros] if offset == 0 else [zeros, flipped]
    lags = jnp.concatenate(pieces, axis=1)
    flat = jnp.tile(lags, (1, kernel))[:, : kernel * (2 * kernel - 1)]
    return flat.reshape(groups, kernel, 2 * kernel - 1)[:, :, kernel - 1 : 2 * kernel - 1]


def apply_blocks(matrix, blocks):
    return jnp.einsum("gts,bsgc->btgc", matrix, blocks, preferred_element_type=jnp.float32)


def body(outer_gate, inner_gate, stream, filters, query_rows, key_rows, *, rows, half):
    row_count, channels = outer_gate.shape
    groups, kernel = filters.shape
    group_size = channels // groups
    seq_span = 2 * half
    ctx_size = rows * half
    in_row = lax.axis_index("col") * CORES + lax.axis_index("core")
    row_index = lax.axis_index("row")
    shard_index = row_index * half + in_row
    seq_place = (shard_index + half) % seq_span
    product = (inner_gate.astype(jnp.float32) * stream.astype(jnp.float32)).astype(jnp.bfloat16)
    blocks = product.reshape(row_count // kernel, kernel, groups, group_size)
    near_taps = toeplitz_taps(filters, 0)
    far_taps = toeplitz_taps(filters, kernel)
    tail_rows = product[row_count - kernel + 1 :]
    earlier = passed_along(tail_rows, CTX_AXES, ctx_size, 1)
    earlier = jnp.where(seq_place == 0, jnp.zeros_like(earlier), earlier)
    first_block = jnp.concatenate([jnp.zeros((1, channels), jnp.bfloat16), earlier], 0)
    first_block = first_block.reshape(1, kernel, groups, group_size)
    before = jnp.concatenate([first_block, blocks[:-1]], 0)
    filtered = (apply_blocks(near_taps, blocks) + apply_blocks(far_taps, before)).reshape(
        row_count, channels
    )
    mixed = (outer_gate.astype(jnp.float32) * filtered).astype(jnp.bfloat16)
    local_heads = channels // HEAD_DIM
    queries = query_rows.reshape(row_count, local_heads, HEAD_DIM)
    score_scale = 1.0 / math.sqrt(HEAD_DIM)
    query_pos = shard_index * row_count + jnp.arange(row_count, dtype=jnp.int32)
    seq_start = jnp.maximum(shard_index - seq_place, 0) * row_count

    kv_rows = jnp.stack([key_rows, mixed])
    from_above = lax.ppermute(kv_rows, "row", [(r, r + 1) for r in range(rows - 1)])
    own_all = lax.all_gather(kv_rows, ("col", "core"), axis=0, tiled=False)
    above_all = lax.all_gather(from_above, ("col", "core"), axis=0, tiled=False)

    def attend(carried, gathered, source_row, first):
        weighted, row_peak, row_total = carried
        window = gathered[first : first + WINDOW_SHARDS]
        key_block = window[:, 0].reshape(WINDOW_SHARDS * row_count, local_heads, HEAD_DIM)
        value_block = window[:, 1].reshape(WINDOW_SHARDS * row_count, local_heads, HEAD_DIM)
        key_start = (source_row * half + first) * row_count
        key_pos = key_start + jnp.arange(WINDOW_SHARDS * row_count, dtype=jnp.int32)
        scores = (
            jnp.einsum("qhd,khd->hqk", queries, key_block, preferred_element_type=jnp.float32)
            * score_scale
        )
        visible_keys = (key_pos[None, :] >= seq_start) & (key_pos[None, :] <= query_pos[:, None])
        scores = jnp.where(visible_keys[None], scores, NEGATIVE)
        new_peak = jnp.maximum(row_peak, jnp.max(scores, axis=2))
        exp_terms = jnp.where(visible_keys[None], jnp.exp(scores - new_peak[..., None]), 0.0)
        rescale = jnp.exp(row_peak - new_peak)
        row_total = row_total * rescale + jnp.sum(exp_terms, axis=2)
        weights = exp_terms.astype(jnp.bfloat16)
        weighted = weighted * rescale[..., None] + jnp.einsum(
            "hqk,khd->hqd", weights, value_block, preferred_element_type=jnp.float32
        )
        return (weighted, new_peak, row_total)

    attn_state = (
        jnp.zeros((local_heads, row_count, HEAD_DIM), jnp.float32),
        jnp.full((local_heads, row_count), NEGATIVE, jnp.float32),
        jnp.zeros((local_heads, row_count), jnp.float32),
    )
    for gathered, source_row in ((own_all, row_index), (above_all, row_index - 1)):
        for first in range(0, half, WINDOW_SHARDS):
            attn_state = attend(attn_state, gathered, source_row, first)
    weighted, row_peak, row_total = attn_state
    attended = (
        (weighted / row_total[..., None])
        .transpose(1, 0, 2)
        .reshape(row_count, channels)
        .astype(jnp.bfloat16)
    )
    return (mixed, attended)


def solution(mesh):
    def run(outer_gate, inner_gate, stream, filters, query_rows, key_rows):
        ctx = mesh.shape["ctx"]
        row_count = outer_gate.shape[0] // ctx
        half = (LENGTH // 2) // row_count
        rows = ctx // half
        devices = mesh.devices.reshape(rows, half // CORES, CORES, mesh.shape["tp"])
        split = Mesh(devices, CTX_AXES + ("tp",))
        rows_spec = P(CTX_AXES, "tp")
        in_specs = (rows_spec, rows_spec, rows_spec, P("tp", None), rows_spec, rows_spec)
        outs = jax.shard_map(
            functools.partial(body, rows=rows, half=half),
            mesh=split,
            in_specs=in_specs,
            out_specs=(rows_spec, rows_spec),
            check_vma=False,
        )(outer_gate, inner_gate, stream, filters, query_rows, key_rows)
        placed = NamedSharding(mesh, P("ctx", "tp"))
        return tuple(lax.with_sharding_constraint(o, placed) for o in outs)

    return run
```

time: 456 us -> 230 us (0.50)
  the two profiles are of different devices: /device:TPU:38 before, /device:TPU:1 now
where the time goes in v2:
time: 230 us; the launch traced here: 229 us
  waiting for transfers between devices  81.6 us (35%)
  local copies, waits for them, and re-layouts  66.8 us (29%)
  matrix products  39.1 us (17%)
  other arithmetic  18.2 us (8%)
  between operations  14.5 us (6%)
  starting transfers between devices  8.69 us (4%)
    all_gather x1, waiting for transfers between devices, body(): own_all = lax.all_gather(kv_rows, ('col', 'core'), axis=0, tiled=False)  43.2 us
    all_gather x1, waiting for transfers between devices, body(): above_all = lax.all_gather(from_above, ('col', 'core'), axis=0, tiled=False)  28.4 us
    dot_general x4, matrix products, attend(): jnp.einsum('qhd,khd->hqk', queries, key_block, preferred_element_type=jnp...  19.4 us
    another operation x4, local copies, waits for them, and re-layouts, attend(): window[:, 1].reshape(WINDOW_SHARDS * row_count, local_heads, HEAD_DIM)  16.1 us
    reshape x2, local copies, waits for them, and re-layouts, toeplitz_taps(): flat.reshape(groups, kernel, 2 * kernel - 1)  15.5 us
    dot_general x4, matrix products, attend(): jnp.einsum('hqk,khd->hqd', weights, value_block, preferred_element_type=j...  15 us
    another operation x4, local copies, waits for them, and re-layouts, attend(): window[:, 0].reshape(WINDOW_SHARDS * row_count, local_heads, HEAD_DIM)  12 us
    reduce_sum x4, other arithmetic, attend(): row_total = row_total * rescale + jnp.sum(exp_terms, axis=2)  11.5 us
  transfers between devices with their start and end apart: 4, of which 3 were waited for; matrix products, arithmetic and copies ran while one was open for 27% of the time, Pallas kernels for 0%

profile of v2, /device:TPU:1, one launch (start us, length us, event | category | flops | bytes accessed | tf_op | source)
XLA Modules:
  0.0 228.9 jit_solution(18048637173813769009)
XLA Ops:
  9.0 5.4 %collective-permute-start = (bf16[127,512]{1,0:T(8,128)(2,1)}, bf16[127,512]{1,0:T(8,128)(2,1)}, u32[]{:S(2)}, u32[]{:S(2)}) collective-permute-start(bf16[127,512]{1,0:T(8,128)(2,1)} %slice.74), channel_id=1, source_target_pairs={{0,4},{4,8},{8,12},{12,16},{16,20},{20,24},{24,28},{28,32},{32,36}... | collective-permute-start | bytes 390152 | tf_op jit(solution)/shard_map/ppermute | solution.py:21
  16.9 7.7 %reshape.314 = bf16[32,128,255]{2,1,0:T(8,128)(2,1)} reshape(bf16[32,32640]{1,0:T(8,128)(2,1)S(1)} %slice.72) | data formatting | bytes 4177920 | tf_op jit(solution)/shard_map/reshape | solution.py:31
  24.7 2.3 %fusion.92 = f32[32,2,16,128]{3,2,1,0:T(8,128)S(1)} fusion(bf16[32,128,255]{2,1,0:T(8,128)(2,1)} %reshape.314, bf16[2,128,32,16]{1,0,3,2:T(2,128)(2,1)S(1)} %reshape.313), kind=kOutput, calls=%fused_computation.59 | convolution fusion | flops 33554432 | bytes 1835008 | tf_op jit(solution)/shard_map/gts,bsgc->btgc/dot_general | solution.py:35
  30.8 7.7 %reshape.316 = bf16[32,128,255]{2,1,0:T(8,128)(2,1)} reshape(bf16[32,32640]{1,0:T(8,128)(2,1)S(1)} %slice.76) | data formatting | bytes 4177920 | tf_op jit(solution)/shard_map/reshape | solution.py:31
  39.8 2.3 %fusion.36 = f32[2,128,32,16]{1,3,0,2:T(8,128)S(1)} fusion(f32[32,2,16,128]{3,2,1,0:T(8,128)S(1)} %fusion.92, bf16[32,128,255]{2,1,0:T(8,128)(2,1)} %reshape.316, bf16[1,128,32,16]{1,3,0,2:T(8,128)(2,1)S(1)} %bitcast.255, bf16[1,128,32,16]{1,3,0,2:T(8,128)(2,1)S(1)} %bitcast.256), kind=kOutput, calls=%fused_computation.45 | convolution fusion | flops 33816576 | bytes 2359296 | tf_op jit(solution)/shard_map/gts,bsgc->btgc/dot_general | solution.py:35
  43.6 3.2 %collective-permute-start.1 = (bf16[2,256,512]{1,2,0:T(8,128)(2,1)S(1)}, bf16[2,256,512]{1,2,0:T(8,128)(2,1)S(1)}, u32[]{:S(2)}, u32[]{:S(2)}) collective-permute-start(bf16[2,256,512]{1,2,0:T(8,128)(2,1)S(1)} %pad_maximum_fusion), channel_id=1, source_target_pairs={{0,64},{64,128},{128,192},{192,256},{256,320},{320,384},{384,448},... | collective-permute-start | bytes 1572872 | tf_op jit(solution)/shard_map/ppermute | solution.py:69
  46.8 9.9 %collective-permute-done.1 = bf16[2,256,512]{1,2,0:T(8,128)(2,1)S(1)} collective-permute-done((bf16[2,256,512]{1,2,0:T(8,128)(2,1)S(1)}, bf16[2,256,512]{1,2,0:T(8,128)(2,1)S(1)}, u32[]{:S(2)}, u32[]{:S(2)}) %collective-permute-start.1) | collective-permute-done | bytes 524320 | tf_op jit(solution)/shard_map/ppermute | solution.py:69
  57.9 4.5 %compare_and_fusion.1 = (pred[256,2048]{0,1:T(8,128)(4,1)S(1)}, pred[256,2048]{0,1:T(8,128)(4,1)}, pred[256,2048]{0,1:T(8,128)(4,1)S(1)}, pred[256,2048]{0,1:T(8,128)(4,1)}) fusion(s32[256]{0:T(256)S(1)} %iota_add_fusion.4, s32[2048]{0:T(1024)S(1)} %get-tuple-element.44, pred[2048]{0:T(1024)(128)(4,1)S(1)} %get-tuple-element.40, ...), kind=kLoop, calls=%fused_computation.41 | loop fusion | flops 4194304 | bytes 2139136 | tf_op jit(solution)/shard_map/and | solution.py:84
  63.4 43.2 %all-gather.5.cloned.1.call-done = bf16[32,256,512]{2,1,0:T(8,128)(2,1)} async-done(((bf16[2,256,512]{2,1,0:T(8,128)(2,1)}), bf16[32,256,512]{2,1,0:T(8,128)(2,1)}) %all-gather.5.cloned.1.call-update) | async-done | bytes 8388624 | tf_op jit(solution)/shard_map/all_gather | solution.py:70
  106.7 5.7 %fusion.141 = (bf16[8,1,256,512]{3,2,1,0:T(8,128)(2,1)}, bf16[8,1,256,512]{3,2,1,0:T(8,128)(2,1)}, bf16[8,1,256,512]{3,2,1,0:T(8,128)(2,1)}, bf16[8,1,256,512]{3,2,1,0:T(8,128)(2,1)S(1)}) fusion(bf16[16,2,256,512]{3,2,1,0:T(8,128)(2,1)} %bitcast.247), kind=kLoop, calls=%fused_computation.122 | loop fusion | bytes 16777216 | tf_op jit(solution)/shard_map/slice | solution.py:77
  112.3 4.0 %reshape.326 = bf16[2048,4,128]{2,1,0:T(4,128)(2,1)} reshape(bf16[8,1,256,512]{3,2,1,0:T(8,128)(2,1)} %get-tuple-element.18) | data formatting | bytes 4194304 | tf_op jit(solution)/shard_map/reshape;squeeze | solution.py:77
  116.4 3.9 %reshape.325 = bf16[2048,4,128]{2,1,0:T(4,128)(2,1)} reshape(bf16[8,1,256,512]{3,2,1,0:T(8,128)(2,1)} %get-tuple-element.19) | data formatting | bytes 4194304 | tf_op jit(solution)/shard_map/reshape;squeeze | solution.py:76
  120.3 4.0 %reshape.324 = bf16[2048,4,128]{2,1,0:T(4,128)(2,1)} reshape(bf16[8,1,256,512]{3,2,1,0:T(8,128)(2,1)} %get-tuple-element.20) | data formatting | bytes 4194304 | tf_op jit(solution)/shard_map/reshape;squeeze | solution.py:77
  124.4 2.0 reshape.323
  126.4 6.6 %fusion = (f32[4,256]{1,0:T(4,128)S(1)}, f32[4,2048,256]{2,1,0:T(8,128)}) fusion(pred[256,2048]{0,1:T(8,128)(4,1)} %get-tuple-element.30, bf16[2048,4,128]{2,1,0:T(4,128)(2,1)} %reshape.323, bf16[256,512]{1,0:T(8,128)(2,1)S(1)} %copy-done), kind=kOutput, calls=%fused_computation.8 | convolution fusion | flops 543161344 | bytes 11276288 | tf_op jit(solution)/shard_map/qhd,khd->hqk/dot_general | solution.py:81
  133.0 4.8 %fusion.1 = (f32[4,256]{1,0:T(4,128)S(1)}, f32[4,2048,256]{2,1,0:T(8,128)}) fusion(pred[256,2048]{0,1:T(8,128)(4,1)S(1)} %copy-done.10, bf16[2048,4,128]{2,1,0:T(4,128)(2,1)S(1)} %copy-done.5, bf16[256,512]{1,0:T(8,128)(2,1)S(1)} %copy-done), kind=kOutput, calls=%fused_computation.9 | convolution fusion | flops 543161344 | bytes 11276288 | tf_op jit(solution)/shard_map/qhd,khd->hqk/dot_general | solution.py:81
  137.8 28.4 %all-gather.7.cloned.1.call-done = bf16[32,256,512]{2,1,0:T(8,128)(2,1)} async-done(((bf16[2,256,512]{2,1,0:T(8,128)(2,1)}), bf16[32,256,512]{2,1,0:T(8,128)(2,1)}) %all-gather.7.cloned.1.call-update) | async-done | bytes 8388624 | tf_op jit(solution)/shard_map/all_gather | solution.py:71
  166.2 5.7 %fusion.140 = (bf16[8,1,256,512]{3,2,1,0:T(8,128)(2,1)}, bf16[8,1,256,512]{3,2,1,0:T(8,128)(2,1)}, bf16[8,1,256,512]{3,2,1,0:T(8,128)(2,1)}, bf16[8,1,256,512]{3,2,1,0:T(8,128)(2,1)S(1)}) fusion(bf16[16,2,256,512]{3,2,1,0:T(8,128)(2,1)} %bitcast.246), kind=kLoop, calls=%fused_computation.121 | loop fusion | bytes 16777216 | tf_op jit(solution)/shard_map/slice | solution.py:77
  171.9 4.0 %reshape.330 = bf16[2048,4,128]{2,1,0:T(4,128)(2,1)} reshape(bf16[8,1,256,512]{3,2,1,0:T(8,128)(2,1)} %get-tuple-element.14) | data formatting | bytes 4194304 | tf_op jit(solution)/shard_map/reshape;squeeze | solution.py:77
  176.0 4.0 %reshape.329 = bf16[2048,4,128]{2,1,0:T(4,128)(2,1)} reshape(bf16[8,1,256,512]{3,2,1,0:T(8,128)(2,1)} %get-tuple-element.15) | data formatting | bytes 4194304 | tf_op jit(solution)/shard_map/reshape;squeeze | solution.py:76
  180.0 4.0 %reshape.328 = bf16[2048,4,128]{2,1,0:T(4,128)(2,1)} reshape(bf16[8,1,256,512]{3,2,1,0:T(8,128)(2,1)} %get-tuple-element.16) | data formatting | bytes 4194304 | tf_op jit(solution)/shard_map/reshape;squeeze | solution.py:77
  183.9 2.1 reshape.327
  186.0 6.5 %fusion.2 = (f32[4,256]{1,0:T(4,128)S(1)}, f32[4,2048,256]{2,1,0:T(8,128)}) fusion(pred[256,2048]{0,1:T(8,128)(4,1)S(1)} %get-tuple-element.27, bf16[2048,4,128]{2,1,0:T(4,128)(2,1)} %reshape.327, bf16[256,512]{1,0:T(8,128)(2,1)S(1)} %copy-done), kind=kOutput, calls=%fused_computation.10 | convolution fusion | flops 543161344 | bytes 11276288 | tf_op jit(solution)/shard_map/qhd,khd->hqk/dot_general | solution.py:81
  192.5 1.5 fusion.3
  194.1 2.1 fusion.10
  196.2 5.0 %fusion.8 = f32[4,256]{1,0:T(4,128)S(1)} fusion(f32[4,2048,256]{2,1,0:T(8,128)} %get-tuple-element.34, f32[4,256]{1,0:T(4,128)S(1)} %get-tuple-element.12, pred[256,2048]{0,1:T(8,128)(4,1)S(1)} %get-tuple-element.27), kind=kLoop, calls=%fused_computation.16 | loop fusion | flops 10484736 | bytes 8921088 | tf_op jit(solution)/shard_map/reduce_sum | solution.py:89
  201.5 2.1 fusion.6
  203.6 2.3 %fusion.4 = f32[4,256]{1,0:T(4,128)S(1)} fusion(f32[4,2048,256]{2,1,0:T(8,128)S(1)} %bitcast.243, f32[4,256]{1,0:T(4,128)S(1)} %get-tuple-element.26, pred[256,2048]{0,1:T(8,128)(4,1)S(1)} %copy-done.12), kind=kLoop, calls=%fused_computation.12 | loop fusion | flops 10484736 | bytes 8921088 | tf_op jit(solution)/shard_map/reduce_sum | solution.py:89
  206.0 5.3 %fusion.87 = f32[256,4,128]{0,2,1:T(8,128)} fusion(f32[4,2048,256]{2,1,0:T(8,128)S(1)} %bitcast.243, f32[4,256]{1,0:T(4,128)S(1)} %get-tuple-element.26, pred[256,2048]{0,1:T(8,128)(4,1)} %get-tuple-element.30, bf16[2048,4,128]{2,1,0:T(4,128)(2,1)} %reshape.324, f32[256,4]{0,1:T(4,128)S(1)} %get-tuple-element.22, f32[256,4]{0,1:T(4,128)S(1)} %get-tuple-element.25), kind=kOutput, calls=%fused_computation.56 | convolution fusion | flops 547618816 | bytes 11546624 | tf_op jit(solution)/shard_map/hqk,khd->hqd/dot_general | solution.py:91
  211.3 4.1 %fusion.77 = f32[256,4,128]{0,2,1:T(8,128)S(1)} fusion(f32[256,4,128]{0,2,1:T(8,128)} %fusion.87, f32[4,2048,256]{2,1,0:T(8,128)S(1)} %bitcast.241, f32[4,256]{1,0:T(4,128)S(1)} %get-tuple-element.13, pred[256,2048]{0,1:T(8,128)(4,1)} %get-tuple-element.28, bf16[2048,4,128]{2,1,0:T(4,128)(2,1)S(1)} %copy-done.1, f32[256,4]{0,1:T(4,128)S(1)} %get-tuple-element.10), kind=kOutput, calls=%fused_computation.54 | convolution fusion | flops 547618816 | bytes 12066816 | tf_op jit(solution)/shard_map/hqk,khd->hqd/dot_general | solution.py:91
  215.5 2.8 %fusion.67 = f32[256,4,128]{0,2,1:T(8,128)S(1)} fusion(f32[256,4,128]{0,2,1:T(8,128)S(1)} %fusion.77, f32[4,2048,256]{2,1,0:T(8,128)S(1)} %bitcast.245, f32[4,256]{1,0:T(4,128)S(1)} %get-tuple-element.12, pred[256,2048]{0,1:T(8,128)(4,1)S(1)} %copy-done.9, bf16[2048,4,128]{2,1,0:T(4,128)(2,1)S(1)} %copy-done.3, f32[256,4]{0,1:T(4,128)S(1)} %get-tuple-element.9), kind=kOutput, calls=%fused_computation.52 | convolution fusion | flops 547618816 | bytes 12066816 | tf_op jit(solution)/shard_map/hqk,khd->hqd/dot_general | solution.py:91
  218.4 2.8 %fusion.98 = bf16[256,4,128]{0,2,1:T(8,128)(2,1)S(1)} fusion(f32[256,4,128]{0,2,1:T(8,128)S(1)} %fusion.67, f32[4,2048,256]{2,1,0:T(8,128)S(1)} %get-tuple-element.32, f32[4,256]{1,0:T(4,128)S(1)} %get-tuple-element.11, pred[256,2048]{0,1:T(8,128)(4,1)S(1)} %copy-done.7, bf16[2048,4,128]{2,1,0:T(4,128)(2,1)S(1)} %copy-done.2, f32[256,4]{0,1:T(4,128)S(1)} %get-tuple-element.8), kind=kOutput, calls=%fused_computation.61 | convolution fusion | flops 547749888 | bytes 11804672 | tf_op jit(solution)/shard_map/hqk,khd->hqd/dot_general | solution.py:91
  (79 shorter events, 14.1 us)
Async XLA Ops:
  7.2 119.2 %copy-start = (bf16[256,512]{1,0:T(8,128)(2,1)S(1)}, bf16[256,512]{1,0:T(8,128)(2,1)}, u32[]{:S(2)}) copy-start(bf16[256,512]{1,0:T(8,128)(2,1)} %param.10) | copy-start | bytes 786436
  7.2 99.5 %all-gather.5.cloned.1.call-start = ((), (), s32[]{:S(2)}) async-start(), calls=%async_computation | async-start | bytes 8912896 | tf_op jit(solution)/shard_map/all_gather | solution.py:70
  9.0 29.6 %collective-permute-start = (bf16[127,512]{1,0:T(8,128)(2,1)}, bf16[127,512]{1,0:T(8,128)(2,1)}, u32[]{:S(2)}, u32[]{:S(2)}) collective-permute-start(bf16[127,512]{1,0:T(8,128)(2,1)} %slice.74), channel_id=1, source_target_pairs={{0,4},{4,8},{8,12},{12,16},{16,20},{20,24},{24,28},{28,32},{32,36}... | collective-permute-start | bytes 390152 | tf_op jit(solution)/shard_map/ppermute | solution.py:21
  43.5 122.7 %all-gather.7.cloned.1.call-start = ((), (), s32[]{:S(2)}) async-start(), calls=%async_computation.1 | async-start | bytes 8912896 | tf_op jit(solution)/shard_map/all_gather | solution.py:71
  43.6 13.2 %collective-permute-start.1 = (bf16[2,256,512]{1,2,0:T(8,128)(2,1)S(1)}, bf16[2,256,512]{1,2,0:T(8,128)(2,1)S(1)}, u32[]{:S(2)}, u32[]{:S(2)}) collective-permute-start(bf16[2,256,512]{1,2,0:T(8,128)(2,1)S(1)} %pad_maximum_fusion), channel_id=1, source_target_pairs={{0,64},{64,128},{128,192},{192,256},{256,320},{320,384},{384,448},... | collective-permute-start | bytes 1572872 | tf_op jit(solution)/shard_map/ppermute | solution.py:69
  62.4 131.6 %copy-start.6 = (pred[256,2048]{0,1:T(8,128)(4,1)}, pred[256,2048]{0,1:T(8,128)(4,1)S(1)}, u32[]{:S(2)}) copy-start(pred[256,2048]{0,1:T(8,128)(4,1)S(1)} %get-tuple-element.29) | copy-start | bytes 1572868
  62.4 133.8 %copy-start.8 = (pred[256,2048]{0,1:T(8,128)(4,1)}, pred[256,2048]{0,1:T(8,128)(4,1)S(1)}, u32[]{:S(2)}) copy-start(pred[256,2048]{0,1:T(8,128)(4,1)S(1)} %get-tuple-element.27) | copy-start | bytes 1572868
  126.4 6.6 %copy-start.5 = (bf16[2048,4,128]{2,1,0:T(4,128)(2,1)S(1)}, bf16[2048,4,128]{2,1,0:T(4,128)(2,1)}, u32[]{:S(2)}) copy-start(bf16[2048,4,128]{2,1,0:T(4,128)(2,1)} %reshape.325) | copy-start | bytes 6291460
  126.4 6.6 %copy-start.10 = (pred[256,2048]{0,1:T(8,128)(4,1)S(1)}, pred[256,2048]{0,1:T(8,128)(4,1)}, u32[]{:S(2)}) copy-start(pred[256,2048]{0,1:T(8,128)(4,1)} %get-tuple-element.28) | copy-start | bytes 1572868
  186.0 6.5 %copy-start.4 = (bf16[2048,4,128]{2,1,0:T(4,128)(2,1)S(1)}, bf16[2048,4,128]{2,1,0:T(4,128)(2,1)}, u32[]{:S(2)}) copy-start(bf16[2048,4,128]{2,1,0:T(4,128)(2,1)} %reshape.329) | copy-start | bytes 6291460
  194.0 7.2 %slice-start = ((s8[8388608]{0:T(1024)(128)(4,1)}), s8[4194304]{0:T(1024)(128)(4,1)S(1)}, s32[]{:S(2)}) async-start(s8[8388608]{0:T(1024)(128)(4,1)} %bitcast.240), calls=%async_computation.2 | async-start | bytes 8388608
  194.1 7.2 %copy-start.11 = (pred[256,2048]{0,1:T(8,128)(4,1)S(1)}, pred[256,2048]{0,1:T(8,128)(4,1)}, u32[]{:S(2)}) copy-start(pred[256,2048]{0,1:T(8,128)(4,1)} %get-tuple-element.28) | copy-start | bytes 1572868
  194.1 9.5 %slice-start.2 = ((s8[8388608]{0:T(1024)(128)(4,1)}), s8[4194304]{0:T(1024)(128)(4,1)S(1)}, s32[]{:S(2)}) async-start(s8[8388608]{0:T(1024)(128)(4,1)} %bitcast.242), calls=%async_computation.4 | async-start | bytes 8388608
  196.2 5.3 %slice-start.1 = ((s8[8388608]{0:T(1024)(128)(4,1)}), s8[4194304]{0:T(1024)(128)(4,1)S(1)}, s32[]{:S(2)}) async-start(s8[8388608]{0:T(1024)(128)(4,1)} %bitcast.240), calls=%async_computation.3 | async-start | bytes 8388608
  196.2 7.4 %slice-start.3 = ((s8[8388608]{0:T(1024)(128)(4,1)}), s8[4194304]{0:T(1024)(128)(4,1)S(1)}, s32[]{:S(2)}) async-start(s8[8388608]{0:T(1024)(128)(4,1)} %bitcast.242), calls=%async_computation.5 | async-start | bytes 8388608
  196.2 7.4 %copy-start.12 = (pred[256,2048]{0,1:T(8,128)(4,1)S(1)}, pred[256,2048]{0,1:T(8,128)(4,1)}, u32[]{:S(2)}) copy-start(pred[256,2048]{0,1:T(8,128)(4,1)} %get-tuple-element.30) | copy-start | bytes 1572868
  206.0 5.3 %copy-start.1 = (bf16[2048,4,128]{2,1,0:T(4,128)(2,1)S(1)}, bf16[2048,4,128]{2,1,0:T(4,128)(2,1)}, u32[]{:S(2)}) copy-start(bf16[2048,4,128]{2,1,0:T(4,128)(2,1)} %reshape.326) | copy-start | bytes 6291460
  206.0 9.5 %slice-start.4 = ((s8[8388608]{0:T(1024)(128)(4,1)}), s8[4194304]{0:T(1024)(128)(4,1)S(1)}, s32[]{:S(2)}) async-start(s8[8388608]{0:T(1024)(128)(4,1)} %bitcast.244), calls=%async_computation.6 | async-start | bytes 8388608
  211.3 4.2 %slice-start.5 = ((s8[8388608]{0:T(1024)(128)(4,1)}), s8[4194304]{0:T(1024)(128)(4,1)S(1)}, s32[]{:S(2)}) async-start(s8[8388608]{0:T(1024)(128)(4,1)} %bitcast.244), calls=%async_computation.7 | async-start | bytes 8388608
  211.3 4.2 %copy-start.3 = (bf16[2048,4,128]{2,1,0:T(4,128)(2,1)S(1)}, bf16[2048,4,128]{2,1,0:T(4,128)(2,1)}, u32[]{:S(2)}) copy-start(bf16[2048,4,128]{2,1,0:T(4,128)(2,1)} %reshape.328) | copy-start | bytes 6291460
  211.3 4.2 %copy-start.9 = (pred[256,2048]{0,1:T(8,128)(4,1)S(1)}, pred[256,2048]{0,1:T(8,128)(4,1)}, u32[]{:S(2)}) copy-start(pred[256,2048]{0,1:T(8,128)(4,1)} %copy-done.8) | copy-start | bytes 1572868
  215.5 2.8 %copy-start.2 = (bf16[2048,4,128]{2,1,0:T(4,128)(2,1)S(1)}, bf16[2048,4,128]{2,1,0:T(4,128)(2,1)}, u32[]{:S(2)}) copy-start(bf16[2048,4,128]{2,1,0:T(4,128)(2,1)} %reshape.330) | copy-start | bytes 6291460
  215.5 2.8 %copy-start.7 = (pred[256,2048]{0,1:T(8,128)(4,1)S(1)}, pred[256,2048]{0,1:T(8,128)(4,1)}, u32[]{:S(2)}) copy-start(pred[256,2048]{0,1:T(8,128)(4,1)} %copy-done.6) | copy-start | bytes 1572868
Sparse Core Ops, SparseCore 0:
  43.6 62.9 all-gather.4
  108.8 57.3 all-gather.6

commit v3 on v2

--- a/solution.py
+++ b/solution.py
@@ -65,20 +65,32 @@
     query_pos = shard_index * row_count + jnp.arange(row_count, dtype=jnp.int32)
     seq_start = jnp.maximum(shard_index - seq_place, 0) * row_count
 
-    kv_rows = jnp.stack([key_rows, mixed])
-    from_above = lax.ppermute(kv_rows, "row", [(r, r + 1) for r in range(rows - 1)])
-    own_all = lax.all_gather(kv_rows, ("col", "core"), axis=0, tiled=False)
-    above_all = lax.all_gather(from_above, ("col", "core"), axis=0, tiled=False)
+    def by_head(array):
+        return array.reshape(row_count, local_heads, HEAD_DIM).transpose(1, 0, 2)
 
-    def attend(carried, gathered, source_row, first):
+    def row_gather(array):
+        return lax.all_gather(array, ("col", "core"), axis=1, tiled=True)
+
+    def row_down(array):
+        return lax.ppermute(array, "row", [(r, r + 1) for r in range(rows - 1)])
+
+    head_queries = by_head(query_rows)
+    head_keys = by_head(key_rows)
+    head_values = by_head(mixed)
+    keys_own = row_gather(head_keys)
+    keys_above = row_gather(row_down(head_keys))
+    values_own = row_gather(head_values)
+    values_above = row_gather(row_down(head_values))
+    window_rows = WINDOW_SHARDS * row_count
+
+    def attend(carried, keys, values, source_row, first):
         weighted, row_peak, row_total = carried
-        window = gathered[first : first + WINDOW_SHARDS]
-        key_block = window[:, 0].reshape(WINDOW_SHARDS * row_count, local_heads, HEAD_DIM)
-        value_block = window[:, 1].reshape(WINDOW_SHARDS * row_count, local_heads, HEAD_DIM)
+        key_block = keys[:, first * row_count : first * row_count + window_rows]
+        value_block = values[:, first * row_count : first * row_count + window_rows]
         key_start = (source_row * half + first) * row_count
-        key_pos = key_start + jnp.arange(WINDOW_SHARDS * row_count, dtype=jnp.int32)
+        key_pos = key_start + jnp.arange(window_rows, dtype=jnp.int32)
         scores = (
-            jnp.einsum("qhd,khd->hqk", queries, key_block, preferred_element_type=jnp.float32)
+            jnp.einsum("hqd,hkd->hqk", head_queries, key_block, preferred_element_type=jnp.float32)
             * score_scale
         )
         visible_keys = (key_pos[None, :] >= seq_start) & (key_pos[None, :] <= query_pos[:, None])
@@ -89,7 +101,7 @@
         row_total = row_total * rescale + jnp.sum(exp_terms, axis=2)
         weights = exp_terms.astype(jnp.bfloat16)
         weighted = weighted * rescale[..., None] + jnp.einsum(
-            "hqk,khd->hqd", weights, value_block, preferred_element_type=jnp.float32
+            "hqk,hkd->hqd", weights, value_block, preferred_element_type=jnp.float32
         )
         return (weighted, new_peak, row_total)
 
@@ -98,9 +110,10 @@
         jnp.full((local_heads, row_count), NEGATIVE, jnp.float32),
         jnp.zeros((local_heads, row_count), jnp.float32),
     )
-    for gathered, source_row in ((own_all, row_index), (above_all, row_index - 1)):
+    sources = ((keys_own, values_own, row_index), (keys_above, values_above, row_index - 1))
+    for keys, values, source_row in sources:
         for first in range(0, half, WINDOW_SHARDS):
-            attn_state = attend(attn_state, gathered, source_row, first)
+            attn_state = attend(attn_state, keys, values, source_row, first)
     weighted, row_peak, row_total = attn_state
     attended = (
         (weighted / row_total[..., None])

time: 230 us -> 233 us (1.013)
  local copies, waits for them, and re-layouts: 66.8 us -> 28.6 us
  waiting for transfers between devices: 81.6 us -> 114 us
  matrix products: 39.1 us -> 46.9 us
  starting transfers between devices: 8.69 us -> 15.5 us
  other arithmetic: 18.2 us -> 13.6 us
    all_gather x2 -> x4, waiting for transfers between devices: 71.6 us -> 104 us  [row_gather(): return lax.all_gather(array, ('col', 'core'), axis=1, tiled=True)]
    another operation x9 -> x0, local copies, waits for them, and re-layouts: 29.1 us -> none  [the longest x4 16.1 us: attend(): window[:, 1].reshape(WINDOW_SHARDS * row_count, local_heads, HEAD_DIM)]
    slice x2 -> x0, local copies, waits for them, and re-layouts: 11.4 us -> none  [attend(): window[:, 1].reshape(WINDOW_SHARDS * row_count, local_heads, HEAD_DIM)]
    dot_general x8, matrix products: 34.4 us -> 42.1 us  [the longest x4 22 us: attend(): jnp.einsum('hqk,hkd->hqd', weights, value_block, preferred_element_type=j...]
    ppermute x1 -> x2, starting transfers between devices: 3.23 us -> 8.28 us  [row_down(): return lax.ppermute(array, 'row', [(r, r + 1) for r in range(rows - 1)])]
    and x1, other arithmetic: 4.51 us -> 1.48 us  [attend(): (key_pos[None, :] >= seq_start) & (key_pos[None, :] <= query_pos[:, None])]
    unnamed x45 -> x33, local copies, waits for them, and re-layouts: 6.93 us -> 9.5 us
    ppermute x1 -> x2, waiting for transfers between devices: 9.93 us -> 9.76 us  [row_down(): return lax.ppermute(array, 'row', [(r, r + 1) for r in range(rows - 1)])]
  transfers between devices with their start and end apart: 4 -> 7, of which waited for: 3 -> 5; matrix products, arithmetic and copies ran while one was open for 27% -> 31% of each run, Pallas kernels for 0% -> 0%
where the time goes in v3:
time: 233 us
  waiting for transfers between devices  114 us (49%)
  matrix products  46.9 us (20%)
  local copies, waits for them, and re-layouts  28.6 us (12%)
  starting transfers between devices  15.5 us (7%)
  between operations  14.1 us (6%)
  other arithmetic  13.6 us (6%)
    all_gather x4, waiting for transfers between devices, row_gather(): return lax.all_gather(array, ('col', 'core'), axis=1, tiled=True)  104 us
    dot_general x4, matrix products, attend(): jnp.einsum('hqk,hkd->hqd', weights, value_block, preferred_element_type=j...  22 us
    dot_general x4, matrix products, attend(): jnp.einsum('hqd,hkd->hqk', head_queries, key_block, preferred_element_typ...  20.2 us
    reshape x2, local copies, waits for them, and re-layouts, toeplitz_taps(): flat.reshape(groups, kernel, 2 * kernel - 1)  15.5 us
    reduce_sum x4, other arithmetic, attend(): row_total = row_total * rescale + jnp.sum(exp_terms, axis=2)  10.2 us
    ppermute x2, waiting for transfers between devices, row_down(): return lax.ppermute(array, 'row', [(r, r + 1) for r in range(rows - 1)])  9.76 us
    unnamed x33, local copies, waits for them, and re-layouts  9.5 us
    ppermute x2, starting transfers between devices, row_down(): return lax.ppermute(array, 'row', [(r, r + 1) for r in range(rows - 1)])  8.28 us
  transfers between devices with their start and end apart: 7, of which 5 were waited for; matrix products, arithmetic and copies ran while one was open for 31% of the time, Pallas kernels for 0%

profile of v3, /device:TPU:1, one launch (start us, length us, event | category | flops | bytes accessed | tf_op | source)
XLA Modules:
  0.0 232.6 jit_solution(16089985115983224624)
XLA Ops:
  7.2 1.1 copy.21
  8.3 0.8 copy.22
  9.3 4.0 %collective-permute-start.1 = (bf16[4,256,128]{2,1,0:T(8,128)(2,1)}, bf16[4,256,128]{2,1,0:T(8,128)(2,1)S(1)}, u32[]{:S(2)}, u32[]{:S(2)}) collective-permute-start(bf16[4,256,128]{2,1,0:T(8,128)(2,1)} %bitcast.176), channel_id=1, source_target_pairs={{0,64},{64,128},{128,192},{192,256},{256,320},{320,384},{384,448},... | collective-permute-start | bytes 786440 | tf_op jit(solution)/shard_map/ppermute | solution.py:75
  13.3 3.6 %collective-permute-done.1 = bf16[4,256,128]{2,1,0:T(8,128)(2,1)S(1)} collective-permute-done((bf16[4,256,128]{2,1,0:T(8,128)(2,1)}, bf16[4,256,128]{2,1,0:T(8,128)(2,1)S(1)}, u32[]{:S(2)}, u32[]{:S(2)}) %collective-permute-start.1) | collective-permute-done | bytes 262176 | tf_op jit(solution)/shard_map/ppermute | solution.py:75
  17.7 1.1 multiply_convert_fusion
  19.5 7.1 %collective-permute-start = (bf16[127,512]{1,0:T(8,128)(2,1)}, bf16[127,512]{1,0:T(8,128)(2,1)S(1)}, u32[]{:S(2)}, u32[]{:S(2)}) collective-permute-start(bf16[127,512]{1,0:T(8,128)(2,1)} %slice.62), channel_id=1, source_target_pairs={{0,4},{4,8},{8,12},{12,16},{16,20},{20,24},{24,28},{28,32},{32,36}... | collective-permute-start | bytes 390152 | tf_op jit(solution)/shard_map/ppermute | solution.py:21
  27.7 1.2 copy.29
  29.1 7.8 %reshape.320 = bf16[32,128,255]{2,1,0:T(8,128)(2,1)} reshape(bf16[32,32640]{1,0:T(8,128)(2,1)S(1)} %slice.60) | data formatting | bytes 4177920 | tf_op jit(solution)/shard_map/reshape | solution.py:31
  36.8 2.4 %fusion.92 = f32[32,2,16,128]{3,2,1,0:T(8,128)S(1)} fusion(bf16[32,128,255]{2,1,0:T(8,128)(2,1)} %reshape.320, bf16[2,128,32,16]{1,0,3,2:T(2,128)(2,1)S(1)} %reshape.319), kind=kOutput, calls=%fused_computation.59 | convolution fusion | flops 33554432 | bytes 1835008 | tf_op jit(solution)/shard_map/gts,bsgc->btgc/dot_general | solution.py:35
  39.5 1.2 copy.30
  40.9 7.8 %reshape.322 = bf16[32,128,255]{2,1,0:T(8,128)(2,1)} reshape(bf16[32,32640]{1,0:T(8,128)(2,1)S(1)} %slice.64) | data formatting | bytes 4177920 | tf_op jit(solution)/shard_map/reshape | solution.py:31
  49.0 2.4 %fusion.36 = f32[2,128,32,16]{1,3,0,2:T(8,128)S(1)} fusion(f32[32,2,16,128]{3,2,1,0:T(8,128)S(1)} %fusion.92, bf16[32,128,255]{2,1,0:T(8,128)(2,1)} %reshape.322, bf16[1,128,32,16]{1,3,0,2:T(8,128)(2,1)S(1)} %bitcast.178, bf16[1,128,32,16]{1,3,0,2:T(8,128)(2,1)S(1)} %bitcast.179), kind=kOutput, calls=%fused_computation.45 | convolution fusion | flops 33816576 | bytes 2359296 | tf_op jit(solution)/shard_map/gts,bsgc->btgc/dot_general | solution.py:35
  52.6 4.2 %collective-permute-start.2 = (bf16[4,256,128]{1,2,0:T(8,128)(2,1)}, bf16[4,256,128]{1,2,0:T(8,128)(2,1)S(1)}, u32[]{:S(2)}, u32[]{:S(2)}) collective-permute-start(bf16[4,256,128]{1,2,0:T(8,128)(2,1)} %bitcast.173), channel_id=1, source_target_pairs={{0,64},{64,128},{128,192},{192,256},{256,320},{320,384},{384,448},... | collective-permute-start | bytes 786440 | tf_op jit(solution)/shard_map/ppermute | solution.py:75
  56.9 6.2 %collective-permute-done.2 = bf16[4,256,128]{1,2,0:T(8,128)(2,1)S(1)} collective-permute-done((bf16[4,256,128]{1,2,0:T(8,128)(2,1)}, bf16[4,256,128]{1,2,0:T(8,128)(2,1)S(1)}, u32[]{:S(2)}, u32[]{:S(2)}) %collective-permute-start.2) | collective-permute-done | bytes 262176 | tf_op jit(solution)/shard_map/ppermute | solution.py:75
  63.8 1.5 compare_and_fusion.3
  65.2 1.8 copy.23
  67.0 6.7 %fusion.1 = (f32[4,256]{1,0:T(4,128)S(1)}, f32[4,256,2048]{2,1,0:T(8,128)}) fusion(pred[256,2048]{1,0:T(8,128)(4,1)S(1)} %get-tuple-element.18, bf16[4,4096,128]{2,1,0:T(8,128)(2,1)} %all-gather.5.cloned.1.call-done, bf16[256,512]{1,0:T(8,128)(2,1)S(1)} %copy-done), kind=kOutput, calls=%fused_computation.9 | convolution fusion | flops 543161344 | bytes 11276288 | tf_op jit(solution)/shard_map/hqd,hkd->hqk/dot_general | solution.py:93
  73.7 4.9 %fusion = (f32[4,256]{1,0:T(4,128)S(1)}, f32[4,256,2048]{2,1,0:T(8,128)}) fusion(pred[256,2048]{1,0:T(8,128)(4,1)S(1)} %get-tuple-element.17, bf16[4,4096,128]{2,1,0:T(8,128)(2,1)S(1)} %copy-done.8, bf16[256,512]{1,0:T(8,128)(2,1)S(1)} %copy-done), kind=kOutput, calls=%fused_computation.8 | convolution fusion | flops 543161344 | bytes 11276288 | tf_op jit(solution)/shard_map/hqd,hkd->hqk/dot_general | solution.py:93
  78.6 29.9 %all-gather.9.cloned.1.call-done = bf16[4,4096,128]{2,1,0:T(8,128)(2,1)} async-done(((bf16[4,256,128]{2,1,0:T(8,128)(2,1)}), bf16[4,4096,128]{2,1,0:T(8,128)(2,1)}) %all-gather.9.cloned.1.call-update) | async-done | bytes 4194320 | tf_op jit(solution)/shard_map/all_gather | solution.py:72
  108.5 3.5 %fusion.3 = (f32[4,256]{1,0:T(4,128)S(1)}, f32[4,256,2048]{2,1,0:T(8,128)S(1)}) fusion(pred[256,2048]{1,0:T(8,128)(4,1)S(1)} %get-tuple-element.20, bf16[4,4096,128]{2,1,0:T(8,128)(2,1)} %all-gather.9.cloned.1.call-done, bf16[256,512]{1,0:T(8,128)(2,1)S(1)} %copy-done), kind=kOutput, calls=%fused_computation.11 | convolution fusion | flops 543161344 | bytes 11276288 | tf_op jit(solution)/shard_map/hqd,hkd->hqk/dot_general | solution.py:93
  112.0 5.1 %fusion.2 = (f32[4,256]{1,0:T(4,128)S(1)}, f32[4,256,2048]{2,1,0:T(8,128)S(1)}) fusion(pred[256,2048]{1,0:T(8,128)(4,1)S(1)} %get-tuple-element.19, bf16[4,4096,128]{2,1,0:T(8,128)(2,1)} %all-gather.9.cloned.1.call-done, bf16[256,512]{1,0:T(8,128)(2,1)S(1)} %copy-done), kind=kOutput, calls=%fused_computation.10 | convolution fusion | flops 543161344 | bytes 11276288 | tf_op jit(solution)/shard_map/hqd,hkd->hqk/dot_general | solution.py:93
  117.1 2.7 %fusion.4 = f32[4,256]{1,0:T(4,128)S(1)} fusion(f32[4,256,2048]{2,1,0:T(8,128)S(1)} %copy-done.4, f32[4,256]{1,0:T(4,128)S(1)} %get-tuple-element.16, pred[256,2048]{1,0:T(8,128)(4,1)S(1)} %get-tuple-element.17), kind=kLoop, calls=%fused_computation.12 | loop fusion | flops 10484736 | bytes 8921088 | tf_op jit(solution)/shard_map/reduce_sum | solution.py:101
  119.9 1.6 slice-done.1
  121.5 2.5 %fusion.6 = f32[4,256]{1,0:T(4,128)S(1)} fusion(f32[4,256,2048]{2,1,0:T(8,128)S(1)} %bitcast.167, f32[4,256]{1,0:T(4,128)S(1)} %get-tuple-element.11, pred[256,2048]{1,0:T(8,128)(4,1)S(1)} %get-tuple-element.18), kind=kLoop, calls=%fused_computation.14 | loop fusion | flops 10484736 | bytes 8921088 | tf_op jit(solution)/shard_map/reduce_sum | solution.py:101
  123.9 2.5 %fusion.8 = f32[4,256]{1,0:T(4,128)S(1)} fusion(f32[4,256,2048]{2,1,0:T(8,128)S(1)} %get-tuple-element.24, f32[4,256]{1,0:T(4,128)S(1)} %get-tuple-element.10, pred[256,2048]{1,0:T(8,128)(4,1)S(1)} %get-tuple-element.19), kind=kLoop, calls=%fused_computation.16 | loop fusion | flops 10484736 | bytes 8921088 | tf_op jit(solution)/shard_map/reduce_sum | solution.py:101
  126.5 2.5 %fusion.10 = f32[4,256]{1,0:T(4,128)S(1)} fusion(f32[4,256,2048]{2,1,0:T(8,128)S(1)} %get-tuple-element.22, f32[4,256]{1,0:T(4,128)S(1)} %get-tuple-element.9, pred[256,2048]{1,0:T(8,128)(4,1)S(1)} %get-tuple-element.20), kind=kLoop, calls=%fused_computation.18 | loop fusion | flops 10484736 | bytes 8921088 | tf_op jit(solution)/shard_map/reduce_sum | solution.py:101
  129.0 31.9 %all-gather.7.cloned.1.call-done = bf16[4,4096,128]{1,2,0:T(8,128)(2,1)} async-done(((bf16[4,256,128]{1,2,0:T(8,128)(2,1)}), bf16[4,4096,128]{1,2,0:T(8,128)(2,1)}) %all-gather.7.cloned.1.call-update) | async-done | bytes 4194320 | tf_op jit(solution)/shard_map/all_gather | solution.py:72
  160.9 5.8 %fusion.87 = f32[256,4,128]{0,2,1:T(8,128)S(1)} fusion(bf16[4,4096,128]{1,2,0:T(8,128)(2,1)} %all-gather.7.cloned.1.call-done, f32[4,256,2048]{2,1,0:T(8,128)} %get-tuple-element.28, f32[4,256]{1,0:T(4,128)S(1)} %get-tuple-element.16, pred[256,2048]{1,0:T(8,128)(4,1)S(1)} %get-tuple-element.17, f32[256,4]{0,1:T(4,128)S(1)} %get-tuple-element.12, ...), kind=kOutput, calls=%fused_computation.56 | convolution fusion | flops 547618816 | bytes 11546624 | tf_op jit(solution)/shard_map/hqk,hkd->hqd/dot_general | solution.py:103
  166.7 4.7 %fusion.77 = f32[256,4,128]{0,2,1:T(8,128)S(1)} fusion(f32[256,4,128]{0,2,1:T(8,128)S(1)} %fusion.87, bf16[4,4096,128]{1,2,0:T(8,128)(2,1)S(1)} %copy-done.9, f32[4,256,2048]{2,1,0:T(8,128)} %get-tuple-element.26, f32[4,256]{1,0:T(4,128)S(1)} %get-tuple-element.11, pred[256,2048]{1,0:T(8,128)(4,1)S(1)} %get-tuple-element.18, f32[256,4]{0,1:T(4,128)S(1)} %get-tuple-element.8), kind=kOutput, calls=%fused_computation.54 | convolution fusion | flops 547618816 | bytes 12066816 | tf_op jit(solution)/shard_map/hqk,hkd->hqd/dot_general | solution.py:103
  171.4 42.3 %all-gather.11.cloned.1.call-done = bf16[4,4096,128]{1,2,0:T(8,128)(2,1)} async-done(((bf16[4,256,128]{1,2,0:T(8,128)(2,1)}), bf16[4,4096,128]{1,2,0:T(8,128)(2,1)}) %all-gather.11.cloned.1.call-update) | async-done | bytes 4194320 | tf_op jit(solution)/shard_map/all_gather | solution.py:72
  213.8 5.6 %fusion.52 = f32[256,4,128]{0,2,1:T(8,128)S(1)} fusion(bf16[4,4096,128]{1,2,0:T(8,128)(2,1)} %all-gather.11.cloned.1.call-done, f32[4,256,2048]{2,1,0:T(8,128)} %copy-done.3, f32[4,256]{1,0:T(4,128)S(1)} %get-tuple-element.9, pred[256,2048]{1,0:T(8,128)(4,1)S(1)} %get-tuple-element.20), kind=kOutput, calls=%fused_computation.49 | convolution fusion | flops 547356672 | bytes 11538432 | tf_op jit(solution)/shard_map/hqk,hkd->hqd/dot_general | solution.py:103
  219.4 5.9 %fusion.98 = bf16[256,4,128]{0,2,1:T(8,128)(2,1)S(1)} fusion(f32[256,4,128]{0,2,1:T(8,128)S(1)} %fusion.52, f32[256,4,128]{0,2,1:T(8,128)S(1)} %fusion.77, bf16[4,4096,128]{1,2,0:T(8,128)(2,1)S(1)} %copy-done.10, f32[4,256,2048]{2,1,0:T(8,128)} %copy-done.2, f32[4,256]{1,0:T(4,128)S(1)} %get-tuple-element.10, pred[256,2048]{1,0:T(8,128)(4,1)S(1)} %get-tuple-element.19, ...), kind=kOutput, calls=%fused_computation.61 | convolution fusion | flops 548012032 | bytes 12333056 | tf_op jit(solution)/shard_map/hqk,hkd->hqd/dot_general | solution.py:103
  (61 shorter events, 6.4 us)
Async XLA Ops:
  7.2 59.9 %copy-start = (bf16[256,512]{1,0:T(8,128)(2,1)S(1)}, bf16[256,512]{1,0:T(8,128)(2,1)}, u32[]{:S(2)}) copy-start(bf16[256,512]{1,0:T(8,128)(2,1)} %param.10) | copy-start | bytes 786436
  7.2 59.9 %all-gather.5.cloned.1.call-start = ((), (), s32[]{:S(2)}) async-start(), calls=%async_computation | async-start | bytes 4456448 | tf_op jit(solution)/shard_map/all_gather | solution.py:72
  9.2 99.3 %all-gather.9.cloned.1.call-start = ((), (), s32[]{:S(2)}) async-start(), calls=%async_computation.2 | async-start | bytes 4456448 | tf_op jit(solution)/shard_map/all_gather | solution.py:72
  9.3 7.7 %collective-permute-start.1 = (bf16[4,256,128]{2,1,0:T(8,128)(2,1)}, bf16[4,256,128]{2,1,0:T(8,128)(2,1)S(1)}, u32[]{:S(2)}, u32[]{:S(2)}) collective-permute-start(bf16[4,256,128]{2,1,0:T(8,128)(2,1)} %bitcast.176), channel_id=1, source_target_pairs={{0,64},{64,128},{128,192},{192,256},{256,320},{320,384},{384,448},... | collective-permute-start | bytes 786440 | tf_op jit(solution)/shard_map/ppermute | solution.py:75
  16.9 0.7 copy-start.6
  17.7 143.2 %all-gather.7.cloned.1.call-start = ((), (), s32[]{:S(2)}) async-start(), calls=%async_computation.1 | async-start | bytes 4456448 | tf_op jit(solution)/shard_map/all_gather | solution.py:72
  19.5 29.3 %collective-permute-start = (bf16[127,512]{1,0:T(8,128)(2,1)}, bf16[127,512]{1,0:T(8,128)(2,1)S(1)}, u32[]{:S(2)}, u32[]{:S(2)}) collective-permute-start(bf16[127,512]{1,0:T(8,128)(2,1)} %slice.62), channel_id=1, source_target_pairs={{0,4},{4,8},{8,12},{12,16},{16,20},{20,24},{24,28},{28,32},{32,36}... | collective-permute-start | bytes 390152 | tf_op jit(solution)/shard_map/ppermute | solution.py:21
  39.2 9.4 %copy-start.5 = (bf16[256,512]{1,0:T(8,128)(2,1)S(1)}, bf16[256,512]{1,0:T(8,128)(2,1)}, u32[]{:S(2)}) copy-start(bf16[256,512]{1,0:T(8,128)(2,1)} %param.6) | copy-start | bytes 786436
  52.5 161.3 %all-gather.11.cloned.1.call-start = ((), (), s32[]{:S(2)}) async-start(), calls=%async_computation.3 | async-start | bytes 4456448 | tf_op jit(solution)/shard_map/all_gather | solution.py:72
  52.6 10.4 %collective-permute-start.2 = (bf16[4,256,128]{1,2,0:T(8,128)(2,1)}, bf16[4,256,128]{1,2,0:T(8,128)(2,1)S(1)}, u32[]{:S(2)}, u32[]{:S(2)}) collective-permute-start(bf16[4,256,128]{1,2,0:T(8,128)(2,1)} %bitcast.173), channel_id=1, source_target_pairs={{0,64},{64,128},{128,192},{192,256},{256,320},{320,384},{384,448},... | collective-permute-start | bytes 786440 | tf_op jit(solution)/shard_map/ppermute | solution.py:75
  63.0 0.7 copy-start.7
  67.0 6.7 %copy-start.8 = (bf16[4,4096,128]{2,1,0:T(8,128)(2,1)S(1)}, bf16[4,4096,128]{2,1,0:T(8,128)(2,1)}, u32[]{:S(2)}) copy-start(bf16[4,4096,128]{2,1,0:T(8,128)(2,1)} %all-gather.5.cloned.1.call-done) | copy-start | bytes 12582916
  108.5 8.6 %copy-start.4 = (f32[4,256,2048]{2,1,0:T(8,128)S(1)}, f32[4,256,2048]{2,1,0:T(8,128)}, u32[]{:S(2)}) copy-start(f32[4,256,2048]{2,1,0:T(8,128)} %get-tuple-element.28) | copy-start | bytes 25165828
  112.0 14.5 %copy-start.3 = (f32[4,256,2048]{2,1,0:T(8,128)}, f32[4,256,2048]{2,1,0:T(8,128)S(1)}, u32[]{:S(2)}) copy-start(f32[4,256,2048]{2,1,0:T(8,128)S(1)} %get-tuple-element.22) | copy-start | bytes 25165828
  112.0 7.9 %slice-start = ((s8[8388608]{0:T(1024)(128)(4,1)}), s8[4194304]{0:T(1024)(128)(4,1)S(1)}, s32[]{:S(2)}) async-start(s8[8388608]{0:T(1024)(128)(4,1)} %bitcast.166), calls=%async_computation.4 | async-start | bytes 8388608
  112.0 9.4 %slice-start.1 = ((s8[8388608]{0:T(1024)(128)(4,1)}), s8[4194304]{0:T(1024)(128)(4,1)S(1)}, s32[]{:S(2)}) async-start(s8[8388608]{0:T(1024)(128)(4,1)} %bitcast.166), calls=%async_computation.5 | async-start | bytes 8388608
  117.1 6.8 %copy-start.2 = (f32[4,256,2048]{2,1,0:T(8,128)}, f32[4,256,2048]{2,1,0:T(8,128)S(1)}, u32[]{:S(2)}) copy-start(f32[4,256,2048]{2,1,0:T(8,128)S(1)} %get-tuple-element.24) | copy-start | bytes 25165828
  160.9 5.8 %copy-start.9 = (bf16[4,4096,128]{1,2,0:T(8,128)(2,1)S(1)}, bf16[4,4096,128]{1,2,0:T(8,128)(2,1)}, u32[]{:S(2)}) copy-start(bf16[4,4096,128]{1,2,0:T(8,128)(2,1)} %all-gather.7.cloned.1.call-done) | copy-start | bytes 12582916
  213.8 5.6 %copy-start.10 = (bf16[4,4096,128]{1,2,0:T(8,128)(2,1)S(1)}, bf16[4,4096,128]{1,2,0:T(8,128)(2,1)}, u32[]{:S(2)}) copy-start(bf16[4,4096,128]{1,2,0:T(8,128)(2,1)} %all-gather.11.cloned.1.call-done) | copy-start | bytes 12582916
  219.3 6.8 %copy-start.1 = (bf16[256,512]{1,0:T(8,128)(2,1)S(1)}, bf16[256,512]{1,0:T(8,128)(2,1)}, u32[]{:S(2)}) copy-start(bf16[256,512]{1,0:T(8,128)(2,1)} %param.10) | copy-start | bytes 786436
Sparse Core Ops, SparseCore 0:
  10.2 51.4 all-gather.4
  63.8 44.6 all-gather.8
  111.1 49.7 all-gather.6
  162.8 50.9 all-gather.10
